TPU v7x, 512 devices: a whole 4x8x8 slice. The times are simulated.
512 devices in a mesh: ctx: 64 (over y, x, core), head: 8 (over z).
Axes of the slice: x: 4, y: 8, z: 8, core: 2. Of those that a mesh axis runs over, the one named last changes fastest.
Arguments:
- tokens: bfloat16 [65536, 2048], P('ctx', 'head'), may hold values from -6 to 6
- w_qkv: bfloat16 [3, 2048, 2048], P(None, 'ctx', 'head'), may hold values from -0.125 to 0.125
- out_gain: float32 [2048], P('head'), may hold values from 0.25 to 1.75
- seg_ids: int32 [65536], P('ctx'), may hold values from 0 to 15, never falling along the last dimension, each value on 1 to 16384 neighbouring positions
Outputs:
- attended: bfloat16 [65536, 2048], P('ctx', 'head')
Inputs may be any that keep to these rules, and one draw needn't show every extreme that they name: `seg_ids`: segment numbers never fall along the stream; each segment covers 1 to 16384 consecutive tokens, and one covers exactly 16384.
All inputs are finite; a program needn't handle non-finite values.
Results may differ from a plain program's by a relative error of at most 0.012.
Values may be sent and summed in bfloat16 or wider, within the bound.
No kernel may reach another device: no remote copies, remote signals or barrier semaphores. Data moves between devices by JAX's collectives and lax.ppermute only.
A program may use at most 64 MiB of HBM per device.

v0:
```python
import jax
import jax.numpy as jnp
from jax import lax
from jax.sharding import PartitionSpec as P

HEAD_DIM = 128


def passed_along(value, axis, steps):
    count = lax.axis_size(axis)
    leading, last = (max(0, -steps), min(count, count - steps))
    return lax.ppermute(value, axis, [(source, source + steps) for source in range(leading, last)])


def feature_map(values):
    return (jax.nn.elu(values.astype(jnp.float32)) + 1.0).astype(jnp.bfloat16)


def combine(earlier, later):
    first_state, first_tail = earlier
    later_state, later_tail = later
    linked = (first_tail == later_tail) | (later_tail < 0.0)
    return (
        later_state + jnp.where(linked, first_state, 0.0),
        jnp.where(later_tail < 0.0, first_tail, later_tail),
    )


def prepare(projected, segment):
    row_count = segment.shape[0]
    head_count = projected.shape[2] // HEAD_DIM
    queries = feature_map(projected[0]).reshape(row_count, head_count, HEAD_DIM)
    key_map = feature_map(projected[1]).reshape(row_count, head_count, HEAD_DIM)
    values = projected[2].reshape(row_count, head_count, HEAD_DIM)
    seg_float = segment.astype(jnp.float32)
    tail_id = seg_float[-1]
    key_tail = jnp.where((seg_float == tail_id)[:, None, None], key_map, jnp.zeros_like(key_map))
    kv_state = jnp.einsum("thd,the->hde", key_tail, values, preferred_element_type=jnp.float32)
    return (queries, key_map, values, seg_float, kv_state, tail_id)


def complete(queries, key_map, values, seg_float, state_in, tail_in, out_gain):
    row_count, head_count = (queries.shape[0], queries.shape[1])
    state_low = state_in.astype(jnp.bfloat16)
    prefix = jnp.einsum("thd,hde->the", queries, state_low, preferred_element_type=jnp.float32)
    prefix = jnp.where((seg_float == tail_in)[:, None, None], prefix, 0.0)
    block_rows = min(512, row_count)
    positions = jnp.arange(row_count, dtype=jnp.int32)

    def one_block(blk_no):
        first_row = blk_no * block_rows
        query_blk = lax.dynamic_slice_in_dim(queries, first_row, block_rows, 0)
        query_pos = first_row + jnp.arange(block_rows, dtype=jnp.int32)
        query_seg = lax.dynamic_slice_in_dim(seg_float, first_row, block_rows, 0)
        scores = jnp.einsum("bhd,shd->hbs", query_blk, key_map, preferred_element_type=jnp.float32)
        visible = (positions[None, :] <= query_pos[:, None]) & (
            seg_float[None, :] == query_seg[:, None]
        )
        weights = jnp.where(visible[None], scores, 0.0).astype(jnp.bfloat16)
        return jnp.einsum("hbs,she->bhe", weights, values, preferred_element_type=jnp.float32)

    local_part = lax.map(one_block, jnp.arange(row_count // block_rows, dtype=jnp.int32))
    numerator = local_part.reshape(row_count, head_count, HEAD_DIM) + prefix
    inv_norm = lax.rsqrt(jnp.mean(numerator * numerator, axis=-1, keepdims=True) + 1e-05)
    result = numerator * inv_norm * out_gain.reshape(head_count, HEAD_DIM)
    return result.astype(jnp.bfloat16).reshape(row_count, head_count * HEAD_DIM)


def per_device(tokens, w_qkv, out_gain, seg_ids):
    whole = lax.all_gather(tokens, "head", axis=1, tiled=True)
    projected = jnp.einsum(
        "tr,grc->gtc",
        whole,
        lax.all_gather(w_qkv, "ctx", axis=1, tiled=True),
        preferred_element_type=jnp.float32,
    ).astype(jnp.bfloat16)
    queries, key_map, values, seg_float, kv_state, tail_id = prepare(projected, seg_ids)
    empty_state = jnp.zeros_like(kv_state)
    own_pair = (kv_state, tail_id)

    def hand_round(turn_no, carried):
        running, _ = carried
        incoming = (
            passed_along(running[0].astype(jnp.bfloat16), "ctx", 1).astype(jnp.float32),
            passed_along(running[1].astype(jnp.bfloat16), "ctx", 1).astype(jnp.float32),
        )
        return (combine(incoming, own_pair), incoming)

    start_pair = (empty_state, jnp.array(-1.0, jnp.float32))
    _, arrived = lax.fori_loop(0, lax.axis_size("ctx") - 1, hand_round, (own_pair, start_pair))
    state_in, tail_in = arrived
    return complete(queries, key_map, values, seg_float, state_in, tail_in, out_gain)


def solution(mesh):
    placed = (P("ctx", "head"), P(None, "ctx", "head"), P("head"), P("ctx"))
    return jax.shard_map(
        per_device, mesh=mesh, in_specs=placed, out_specs=P("ctx", "head"), check_vma=False
    )
```

profile of v0, /device:TPU:32, one launch (start us, length us, event | category | flops | bytes accessed | tf_op | source)
XLA Modules:
  0.0 1084.5 jit_solution(1804793181118891656)
XLA Ops:
  12.1 84.4 %all-gather.3.cloned.1.call-done = bf16[3,2048,256]{2,1,0:T(8,128)(2,1)} async-done(((bf16[3,32,256]{2,1,0:T(8,128)(2,1)}), bf16[3,2048,256]{2,1,0:T(8,128)(2,1)}) %all-gather.3.cloned.1.call-update) | async-done | bytes 3145744 | tf_op jit(solution)/shard_map/all_gather | solution.py:74
  96.5 67.6 %all-gather.5.cloned.1.call-done = bf16[1024,2048]{1,0:T(8,128)(2,1)} async-done(((bf16[1024,256]{1,0:T(8,128)(2,1)}), bf16[1024,2048]{1,0:T(8,128)(2,1)}) %all-gather.5.cloned.1.call-update) | async-done | bytes 4194320 | tf_op jit(solution)/shard_map/all_gather | solution.py:70
  164.0 6.6 fusion.15
  176.5 877.2 %while.28 = (s32[]{:T(128)}, bf16[2,128,128]{2,1,0:T(8,128)(2,1)S(1)}, bf16[]{:T(256)}, bf16[2,128,128]{2,1,0:T(8,128)(2,1)}, f32[]{:T(128)}, /*index=5*/f32[]{:...) while((s32[]{:T(128)}, bf16[2,128,128]{2,1,0:T(8,128)(2,1)S(1)}, bf16[]{:T(256)}, ...), condition=%wide.region_3.4_spmd, body=%wide.region_2.3_spmd.sunk | while | flops 163846 | bytes 590031 | solution.py:90
  195.3 5.4 collective-permute-done
  209.2 5.4 collective-permute-done
  223.1 5.4 collective-permute-done
  237.0 5.4 collective-permute-done
  250.9 5.4 collective-permute-done
  264.9 5.4 collective-permute-done
  278.8 5.4 collective-permute-done
  292.7 5.4 collective-permute-done
  306.6 5.4 collective-permute-done
  320.6 5.4 collective-permute-done
  334.5 5.4 collective-permute-done
  348.4 5.4 collective-permute-done
  362.3 5.4 collective-permute-done
  376.3 5.4 collective-permute-done
  390.2 5.4 collective-permute-done
  404.1 5.4 collective-permute-done
  418.0 5.4 collective-permute-done
  432.0 5.4 collective-permute-done
  445.9 5.4 collective-permute-done
  459.8 5.4 collective-permute-done
  473.7 5.4 collective-permute-done
  487.6 5.4 collective-permute-done
  501.6 5.4 collective-permute-done
  515.5 5.4 collective-permute-done
  529.4 5.4 collective-permute-done
  543.3 5.4 collective-permute-done
  557.3 5.4 collective-permute-done
  571.2 5.4 collective-permute-done
  585.1 5.4 collective-permute-done
  599.0 5.4 collective-permute-done
  613.0 5.4 collective-permute-done
  626.9 5.4 collective-permute-done
  640.8 5.4 collective-permute-done
  654.7 5.4 collective-permute-done
  668.6 5.4 collective-permute-done
  682.6 5.4 collective-permute-done
  696.5 5.4 collective-permute-done
  710.4 5.4 collective-permute-done
  724.3 5.4 collective-permute-done
  738.3 5.4 collective-permute-done
  752.2 5.4 collective-permute-done
  766.1 5.4 collective-permute-done
  780.0 5.4 collective-permute-done
  794.0 5.4 collective-permute-done
  807.9 5.4 collective-permute-done
  821.8 5.4 collective-permute-done
  835.7 5.4 collective-permute-done
  849.6 5.4 collective-permute-done
  863.6 5.4 collective-permute-done
  877.5 5.4 collective-permute-done
  891.4 5.4 collective-permute-done
  905.3 5.4 collective-permute-done
  933.2 5.4 collective-permute-done
  947.1 5.4 collective-permute-done
  961.0 5.4 collective-permute-done
  975.0 5.4 collective-permute-done
  988.9 5.4 collective-permute-done
  1002.8 5.4 collective-permute-done
  1016.7 5.4 collective-permute-done
  1056.0 19.2 %while.29 = (s32[]{:T(128)}, f32[2,512,2,128]{1,0,3,2:T(2,128)S(1)}, s32[2]{0:T(128)S(1)}, f32[1024]{0:T(1024)S(1)}, bf16[1024,2,128]{2,1,0:T(2,128)(2,1)S(1)}, ...) while((s32[]{:T(128)}, ...), condition=%wide.region_1.2_spmd.clone, body=%wide.region_0.1_spmd.clone.sunk | while | flops 540541440 | bytes 5519551 | solution.py:62
  (303 shorter events, 395.1 us)
Async XLA Ops:
  6.5 89.9 %all-gather.3.cloned.1.call-start = ((), (), s32[]{:S(2)}) async-start(), calls=%async_computation | async-start | bytes 3194880 | tf_op jit(solution)/shard_map/all_gather | solution.py:74
  7.3 156.8 %all-gather.5.cloned.1.call-start = ((), (), s32[]{:S(2)}) async-start(), calls=%async_computation.1 | async-start | bytes 4718592 | tf_op jit(solution)/shard_map/all_gather | solution.py:70
  176.5 13.3 %collective-permute-start.1 = (bf16[2,128,128]{2,1,0:T(8,128)(2,1)S(1)}, bf16[2,128,128]{2,1,0:T(8,128)(2,1)S(1)}, u32[]{:S(2)}, u32[]{:S(2)}) collective-permute-start(bf16[2,128,128]{2,1,0:T(8,128)(2,1)S(1)} %get-tuple-element.318), channel_id=1, source_target_pairs={{0,8},{8,16},{16,24},{24,32},{32,40},{40,48},{48,56},{56,64},{64,7... | collective-permute-start | bytes 196616 | tf_op jit(solution)/shard_map/while/body/eval_jaxpr/ppermute | solution.py:12
  190.5 13.3 %collective-permute-start.1 = (bf16[2,128,128]{2,1,0:T(8,128)(2,1)S(1)}, bf16[2,128,128]{2,1,0:T(8,128)(2,1)S(1)}, u32[]{:S(2)}, u32[]{:S(2)}) collective-permute-start(bf16[2,128,128]{2,1,0:T(8,128)(2,1)S(1)} %get-tuple-element.318), channel_id=1, source_target_pairs={{0,8},{8,16},{16,24},{24,32},{32,40},{40,48},{48,56},{56,64},{64,7... | collective-permute-start | bytes 196616 | tf_op jit(solution)/shard_map/while/body/eval_jaxpr/ppermute | solution.py:12
  204.4 13.3 %collective-permute-start.1 = (bf16[2,128,128]{2,1,0:T(8,128)(2,1)S(1)}, bf16[2,128,128]{2,1,0:T(8,128)(2,1)S(1)}, u32[]{:S(2)}, u32[]{:S(2)}) collective-permute-start(bf16[2,128,128]{2,1,0:T(8,128)(2,1)S(1)} %get-tuple-element.318), channel_id=1, source_target_pairs={{0,8},{8,16},{16,24},{24,32},{32,40},{40,48},{48,56},{56,64},{64,7... | collective-permute-start | bytes 196616 | tf_op jit(solution)/shard_map/while/body/eval_jaxpr/ppermute | solution.py:12
  218.3 13.3 %collective-permute-start.1 = (bf16[2,128,128]{2,1,0:T(8,128)(2,1)S(1)}, bf16[2,128,128]{2,1,0:T(8,128)(2,1)S(1)}, u32[]{:S(2)}, u32[]{:S(2)}) collective-permute-start(bf16[2,128,128]{2,1,0:T(8,128)(2,1)S(1)} %get-tuple-element.318), channel_id=1, source_target_pairs={{0,8},{8,16},{16,24},{24,32},{32,40},{40,48},{48,56},{56,64},{64,7... | collective-permute-start | bytes 196616 | tf_op jit(solution)/shard_map/while/body/eval_jaxpr/ppermute | solution.py:12
  232.3 13.3 %collective-permute-start.1 = (bf16[2,128,128]{2,1,0:T(8,128)(2,1)S(1)}, bf16[2,128,128]{2,1,0:T(8,128)(2,1)S(1)}, u32[]{:S(2)}, u32[]{:S(2)}) collective-permute-start(bf16[2,128,128]{2,1,0:T(8,128)(2,1)S(1)} %get-tuple-element.318), channel_id=1, source_target_pairs={{0,8},{8,16},{16,24},{24,32},{32,40},{40,48},{48,56},{56,64},{64,7... | collective-permute-start | bytes 196616 | tf_op jit(solution)/shard_map/while/body/eval_jaxpr/ppermute | solution.py:12
  246.2 13.3 %collective-permute-start.1 = (bf16[2,128,128]{2,1,0:T(8,128)(2,1)S(1)}, bf16[2,128,128]{2,1,0:T(8,128)(2,1)S(1)}, u32[]{:S(2)}, u32[]{:S(2)}) collective-permute-start(bf16[2,128,128]{2,1,0:T(8,128)(2,1)S(1)} %get-tuple-element.318), channel_id=1, source_target_pairs={{0,8},{8,16},{16,24},{24,32},{32,40},{40,48},{48,56},{56,64},{64,7... | collective-permute-start | bytes 196616 | tf_op jit(solution)/shard_map/while/body/eval_jaxpr/ppermute | solution.py:12
  260.1 13.3 %collective-permute-start.1 = (bf16[2,128,128]{2,1,0:T(8,128)(2,1)S(1)}, bf16[2,128,128]{2,1,0:T(8,128)(2,1)S(1)}, u32[]{:S(2)}, u32[]{:S(2)}) collective-permute-start(bf16[2,128,128]{2,1,0:T(8,128)(2,1)S(1)} %get-tuple-element.318), channel_id=1, source_target_pairs={{0,8},{8,16},{16,24},{24,32},{32,40},{40,48},{48,56},{56,64},{64,7... | collective-permute-start | bytes 196616 | tf_op jit(solution)/shard_map/while/body/eval_jaxpr/ppermute | solution.py:12
  274.0 13.3 %collective-permute-start.1 = (bf16[2,128,128]{2,1,0:T(8,128)(2,1)S(1)}, bf16[2,128,128]{2,1,0:T(8,128)(2,1)S(1)}, u32[]{:S(2)}, u32[]{:S(2)}) collective-permute-start(bf16[2,128,128]{2,1,0:T(8,128)(2,1)S(1)} %get-tuple-element.318), channel_id=1, source_target_pairs={{0,8},{8,16},{16,24},{24,32},{32,40},{40,48},{48,56},{56,64},{64,7... | collective-permute-start | bytes 196616 | tf_op jit(solution)/shard_map/while/body/eval_jaxpr/ppermute | solution.py:12
  287.9 13.3 %collective-permute-start.1 = (bf16[2,128,128]{2,1,0:T(8,128)(2,1)S(1)}, bf16[2,128,128]{2,1,0:T(8,128)(2,1)S(1)}, u32[]{:S(2)}, u32[]{:S(2)}) collective-permute-start(bf16[2,128,128]{2,1,0:T(8,128)(2,1)S(1)} %get-tuple-element.318), channel_id=1, source_target_pairs={{0,8},{8,16},{16,24},{24,32},{32,40},{40,48},{48,56},{56,64},{64,7... | collective-permute-start | bytes 196616 | tf_op jit(solution)/shard_map/while/body/eval_jaxpr/ppermute | solution.py:12
  301.9 13.3 %collective-permute-start.1 = (bf16[2,128,128]{2,1,0:T(8,128)(2,1)S(1)}, bf16[2,128,128]{2,1,0:T(8,128)(2,1)S(1)}, u32[]{:S(2)}, u32[]{:S(2)}) collective-permute-start(bf16[2,128,128]{2,1,0:T(8,128)(2,1)S(1)} %get-tuple-element.318), channel_id=1, source_target_pairs={{0,8},{8,16},{16,24},{24,32},{32,40},{40,48},{48,56},{56,64},{64,7... | collective-permute-start | bytes 196616 | tf_op jit(solution)/shard_map/while/body/eval_jaxpr/ppermute | solution.py:12
  315.8 13.3 %collective-permute-start.1 = (bf16[2,128,128]{2,1,0:T(8,128)(2,1)S(1)}, bf16[2,128,128]{2,1,0:T(8,128)(2,1)S(1)}, u32[]{:S(2)}, u32[]{:S(2)}) collective-permute-start(bf16[2,128,128]{2,1,0:T(8,128)(2,1)S(1)} %get-tuple-element.318), channel_id=1, source_target_pairs={{0,8},{8,16},{16,24},{24,32},{32,40},{40,48},{48,56},{56,64},{64,7... | collective-permute-start | bytes 196616 | tf_op jit(solution)/shard_map/while/body/eval_jaxpr/ppermute | solution.py:12
  329.7 13.3 %collective-permute-start.1 = (bf16[2,128,128]{2,1,0:T(8,128)(2,1)S(1)}, bf16[2,128,128]{2,1,0:T(8,128)(2,1)S(1)}, u32[]{:S(2)}, u32[]{:S(2)}) collective-permute-start(bf16[2,128,128]{2,1,0:T(8,128)(2,1)S(1)} %get-tuple-element.318), channel_id=1, source_target_pairs={{0,8},{8,16},{16,24},{24,32},{32,40},{40,48},{48,56},{56,64},{64,7... | collective-permute-start | bytes 196616 | tf_op jit(solution)/shard_map/while/body/eval_jaxpr/ppermute | solution.py:12
  343.6 13.3 %collective-permute-start.1 = (bf16[2,128,128]{2,1,0:T(8,128)(2,1)S(1)}, bf16[2,128,128]{2,1,0:T(8,128)(2,1)S(1)}, u32[]{:S(2)}, u32[]{:S(2)}) collective-permute-start(bf16[2,128,128]{2,1,0:T(8,128)(2,1)S(1)} %get-tuple-element.318), channel_id=1, source_target_pairs={{0,8},{8,16},{16,24},{24,32},{32,40},{40,48},{48,56},{56,64},{64,7... | collective-permute-start | bytes 196616 | tf_op jit(solution)/shard_map/while/body/eval_jaxpr/ppermute | solution.py:12
  357.6 13.3 %collective-permute-start.1 = (bf16[2,128,128]{2,1,0:T(8,128)(2,1)S(1)}, bf16[2,128,128]{2,1,0:T(8,128)(2,1)S(1)}, u32[]{:S(2)}, u32[]{:S(2)}) collective-permute-start(bf16[2,128,128]{2,1,0:T(8,128)(2,1)S(1)} %get-tuple-element.318), channel_id=1, source_target_pairs={{0,8},{8,16},{16,24},{24,32},{32,40},{40,48},{48,56},{56,64},{64,7... | collective-permute-start | bytes 196616 | tf_op jit(solution)/shard_map/while/body/eval_jaxpr/ppermute | solution.py:12
  371.5 13.3 %collective-permute-start.1 = (bf16[2,128,128]{2,1,0:T(8,128)(2,1)S(1)}, bf16[2,128,128]{2,1,0:T(8,128)(2,1)S(1)}, u32[]{:S(2)}, u32[]{:S(2)}) collective-permute-start(bf16[2,128,128]{2,1,0:T(8,128)(2,1)S(1)} %get-tuple-element.318), channel_id=1, source_target_pairs={{0,8},{8,16},{16,24},{24,32},{32,40},{40,48},{48,56},{56,64},{64,7... | collective-permute-start | bytes 196616 | tf_op jit(solution)/shard_map/while/body/eval_jaxpr/ppermute | solution.py:12
  385.4 13.3 %collective-permute-start.1 = (bf16[2,128,128]{2,1,0:T(8,128)(2,1)S(1)}, bf16[2,128,128]{2,1,0:T(8,128)(2,1)S(1)}, u32[]{:S(2)}, u32[]{:S(2)}) collective-permute-start(bf16[2,128,128]{2,1,0:T(8,128)(2,1)S(1)} %get-tuple-element.318), channel_id=1, source_target_pairs={{0,8},{8,16},{16,24},{24,32},{32,40},{40,48},{48,56},{56,64},{64,7... | collective-permute-start | bytes 196616 | tf_op jit(solution)/shard_map/while/body/eval_jaxpr/ppermute | solution.py:12
  399.3 13.3 %collective-permute-start.1 = (bf16[2,128,128]{2,1,0:T(8,128)(2,1)S(1)}, bf16[2,128,128]{2,1,0:T(8,128)(2,1)S(1)}, u32[]{:S(2)}, u32[]{:S(2)}) collective-permute-start(bf16[2,128,128]{2,1,0:T(8,128)(2,1)S(1)} %get-tuple-element.318), channel_id=1, source_target_pairs={{0,8},{8,16},{16,24},{24,32},{32,40},{40,48},{48,56},{56,64},{64,7... | collective-permute-start | bytes 196616 | tf_op jit(solution)/shard_map/while/body/eval_jaxpr/ppermute | solution.py:12
  413.3 13.3 %collective-permute-start.1 = (bf16[2,128,128]{2,1,0:T(8,128)(2,1)S(1)}, bf16[2,128,128]{2,1,0:T(8,128)(2,1)S(1)}, u32[]{:S(2)}, u32[]{:S(2)}) collective-permute-start(bf16[2,128,128]{2,1,0:T(8,128)(2,1)S(1)} %get-tuple-element.318), channel_id=1, source_target_pairs={{0,8},{8,16},{16,24},{24,32},{32,40},{40,48},{48,56},{56,64},{64,7... | collective-permute-start | bytes 196616 | tf_op jit(solution)/shard_map/while/body/eval_jaxpr/ppermute | solution.py:12
  427.2 13.3 %collective-permute-start.1 = (bf16[2,128,128]{2,1,0:T(8,128)(2,1)S(1)}, bf16[2,128,128]{2,1,0:T(8,128)(2,1)S(1)}, u32[]{:S(2)}, u32[]{:S(2)}) collective-permute-start(bf16[2,128,128]{2,1,0:T(8,128)(2,1)S(1)} %get-tuple-element.318), channel_id=1, source_target_pairs={{0,8},{8,16},{16,24},{24,32},{32,40},{40,48},{48,56},{56,64},{64,7... | collective-permute-start | bytes 196616 | tf_op jit(solution)/shard_map/while/body/eval_jaxpr/ppermute | solution.py:12
  441.1 13.3 %collective-permute-start.1 = (bf16[2,128,128]{2,1,0:T(8,128)(2,1)S(1)}, bf16[2,128,128]{2,1,0:T(8,128)(2,1)S(1)}, u32[]{:S(2)}, u32[]{:S(2)}) collective-permute-start(bf16[2,128,128]{2,1,0:T(8,128)(2,1)S(1)} %get-tuple-element.318), channel_id=1, source_target_pairs={{0,8},{8,16},{16,24},{24,32},{32,40},{40,48},{48,56},{56,64},{64,7... | collective-permute-start | bytes 196616 | tf_op jit(solution)/shard_map/while/body/eval_jaxpr/ppermute | solution.py:12
  455.0 13.3 %collective-permute-start.1 = (bf16[2,128,128]{2,1,0:T(8,128)(2,1)S(1)}, bf16[2,128,128]{2,1,0:T(8,128)(2,1)S(1)}, u32[]{:S(2)}, u32[]{:S(2)}) collective-permute-start(bf16[2,128,128]{2,1,0:T(8,128)(2,1)S(1)} %get-tuple-element.318), channel_id=1, source_target_pairs={{0,8},{8,16},{16,24},{24,32},{32,40},{40,48},{48,56},{56,64},{64,7... | collective-permute-start | bytes 196616 | tf_op jit(solution)/shard_map/while/body/eval_jaxpr/ppermute | solution.py:12
  468.9 13.3 %collective-permute-start.1 = (bf16[2,128,128]{2,1,0:T(8,128)(2,1)S(1)}, bf16[2,128,128]{2,1,0:T(8,128)(2,1)S(1)}, u32[]{:S(2)}, u32[]{:S(2)}) collective-permute-start(bf16[2,128,128]{2,1,0:T(8,128)(2,1)S(1)} %get-tuple-element.318), channel_id=1, source_target_pairs={{0,8},{8,16},{16,24},{24,32},{32,40},{40,48},{48,56},{56,64},{64,7... | collective-permute-start | bytes 196616 | tf_op jit(solution)/shard_map/while/body/eval_jaxpr/ppermute | solution.py:12
  482.9 13.3 %collective-permute-start.1 = (bf16[2,128,128]{2,1,0:T(8,128)(2,1)S(1)}, bf16[2,128,128]{2,1,0:T(8,128)(2,1)S(1)}, u32[]{:S(2)}, u32[]{:S(2)}) collective-permute-start(bf16[2,128,128]{2,1,0:T(8,128)(2,1)S(1)} %get-tuple-element.318), channel_id=1, source_target_pairs={{0,8},{8,16},{16,24},{24,32},{32,40},{40,48},{48,56},{56,64},{64,7... | collective-permute-start | bytes 196616 | tf_op jit(solution)/shard_map/while/body/eval_jaxpr/ppermute | solution.py:12
  496.8 13.3 %collective-permute-start.1 = (bf16[2,128,128]{2,1,0:T(8,128)(2,1)S(1)}, bf16[2,128,128]{2,1,0:T(8,128)(2,1)S(1)}, u32[]{:S(2)}, u32[]{:S(2)}) collective-permute-start(bf16[2,128,128]{2,1,0:T(8,128)(2,1)S(1)} %get-tuple-element.318), channel_id=1, source_target_pairs={{0,8},{8,16},{16,24},{24,32},{32,40},{40,48},{48,56},{56,64},{64,7... | collective-permute-start | bytes 196616 | tf_op jit(solution)/shard_map/while/body/eval_jaxpr/ppermute | solution.py:12
  510.7 13.3 %collective-permute-start.1 = (bf16[2,128,128]{2,1,0:T(8,128)(2,1)S(1)}, bf16[2,128,128]{2,1,0:T(8,128)(2,1)S(1)}, u32[]{:S(2)}, u32[]{:S(2)}) collective-permute-start(bf16[2,128,128]{2,1,0:T(8,128)(2,1)S(1)} %get-tuple-element.318), channel_id=1, source_target_pairs={{0,8},{8,16},{16,24},{24,32},{32,40},{40,48},{48,56},{56,64},{64,7... | collective-permute-start | bytes 196616 | tf_op jit(solution)/shard_map/while/body/eval_jaxpr/ppermute | solution.py:12
  524.6 13.3 %collective-permute-start.1 = (bf16[2,128,128]{2,1,0:T(8,128)(2,1)S(1)}, bf16[2,128,128]{2,1,0:T(8,128)(2,1)S(1)}, u32[]{:S(2)}, u32[]{:S(2)}) collective-permute-start(bf16[2,128,128]{2,1,0:T(8,128)(2,1)S(1)} %get-tuple-element.318), channel_id=1, source_target_pairs={{0,8},{8,16},{16,24},{24,32},{32,40},{40,48},{48,56},{56,64},{64,7... | collective-permute-start | bytes 196616 | tf_op jit(solution)/shard_map/while/body/eval_jaxpr/ppermute | solution.py:12
  538.6 13.3 %collective-permute-start.1 = (bf16[2,128,128]{2,1,0:T(8,128)(2,1)S(1)}, bf16[2,128,128]{2,1,0:T(8,128)(2,1)S(1)}, u32[]{:S(2)}, u32[]{:S(2)}) collective-permute-start(bf16[2,128,128]{2,1,0:T(8,128)(2,1)S(1)} %get-tuple-element.318), channel_id=1, source_target_pairs={{0,8},{8,16},{16,24},{24,32},{32,40},{40,48},{48,56},{56,64},{64,7... | collective-permute-start | bytes 196616 | tf_op jit(solution)/shard_map/while/body/eval_jaxpr/ppermute | solution.py:12
  552.5 13.3 %collective-permute-start.1 = (bf16[2,128,128]{2,1,0:T(8,128)(2,1)S(1)}, bf16[2,128,128]{2,1,0:T(8,128)(2,1)S(1)}, u32[]{:S(2)}, u32[]{:S(2)}) collective-permute-start(bf16[2,128,128]{2,1,0:T(8,128)(2,1)S(1)} %get-tuple-element.318), channel_id=1, source_target_pairs={{0,8},{8,16},{16,24},{24,32},{32,40},{40,48},{48,56},{56,64},{64,7... | collective-permute-start | bytes 196616 | tf_op jit(solution)/shard_map/while/body/eval_jaxpr/ppermute | solution.py:12
  566.4 13.3 %collective-permute-start.1 = (bf16[2,128,128]{2,1,0:T(8,128)(2,1)S(1)}, bf16[2,128,128]{2,1,0:T(8,128)(2,1)S(1)}, u32[]{:S(2)}, u32[]{:S(2)}) collective-permute-start(bf16[2,128,128]{2,1,0:T(8,128)(2,1)S(1)} %get-tuple-element.318), channel_id=1, source_target_pairs={{0,8},{8,16},{16,24},{24,32},{32,40},{40,48},{48,56},{56,64},{64,7... | collective-permute-start | bytes 196616 | tf_op jit(solution)/shard_map/while/body/eval_jaxpr/ppermute | solution.py:12
  580.3 13.3 %collective-permute-start.1 = (bf16[2,128,128]{2,1,0:T(8,128)(2,1)S(1)}, bf16[2,128,128]{2,1,0:T(8,128)(2,1)S(1)}, u32[]{:S(2)}, u32[]{:S(2)}) collective-permute-start(bf16[2,128,128]{2,1,0:T(8,128)(2,1)S(1)} %get-tuple-element.318), channel_id=1, source_target_pairs={{0,8},{8,16},{16,24},{24,32},{32,40},{40,48},{48,56},{56,64},{64,7... | collective-permute-start | bytes 196616 | tf_op jit(solution)/shard_map/while/body/eval_jaxpr/ppermute | solution.py:12
  594.3 13.3 %collective-permute-start.1 = (bf16[2,128,128]{2,1,0:T(8,128)(2,1)S(1)}, bf16[2,128,128]{2,1,0:T(8,128)(2,1)S(1)}, u32[]{:S(2)}, u32[]{:S(2)}) collective-permute-start(bf16[2,128,128]{2,1,0:T(8,128)(2,1)S(1)} %get-tuple-element.318), channel_id=1, source_target_pairs={{0,8},{8,16},{16,24},{24,32},{32,40},{40,48},{48,56},{56,64},{64,7... | collective-permute-start | bytes 196616 | tf_op jit(solution)/shard_map/while/body/eval_jaxpr/ppermute | solution.py:12
  608.2 13.3 %collective-permute-start.1 = (bf16[2,128,128]{2,1,0:T(8,128)(2,1)S(1)}, bf16[2,128,128]{2,1,0:T(8,128)(2,1)S(1)}, u32[]{:S(2)}, u32[]{:S(2)}) collective-permute-start(bf16[2,128,128]{2,1,0:T(8,128)(2,1)S(1)} %get-tuple-element.318), channel_id=1, source_target_pairs={{0,8},{8,16},{16,24},{24,32},{32,40},{40,48},{48,56},{56,64},{64,7... | collective-permute-start | bytes 196616 | tf_op jit(solution)/shard_map/while/body/eval_jaxpr/ppermute | solution.py:12
  622.1 13.3 %collective-permute-start.1 = (bf16[2,128,128]{2,1,0:T(8,128)(2,1)S(1)}, bf16[2,128,128]{2,1,0:T(8,128)(2,1)S(1)}, u32[]{:S(2)}, u32[]{:S(2)}) collective-permute-start(bf16[2,128,128]{2,1,0:T(8,128)(2,1)S(1)} %get-tuple-element.318), channel_id=1, source_target_pairs={{0,8},{8,16},{16,24},{24,32},{32,40},{40,48},{48,56},{56,64},{64,7... | collective-permute-start | bytes 196616 | tf_op jit(solution)/shard_map/while/body/eval_jaxpr/ppermute | solution.py:12
  636.0 13.3 %collective-permute-start.1 = (bf16[2,128,128]{2,1,0:T(8,128)(2,1)S(1)}, bf16[2,128,128]{2,1,0:T(8,128)(2,1)S(1)}, u32[]{:S(2)}, u32[]{:S(2)}) collective-permute-start(bf16[2,128,128]{2,1,0:T(8,128)(2,1)S(1)} %get-tuple-element.318), channel_id=1, source_target_pairs={{0,8},{8,16},{16,24},{24,32},{32,40},{40,48},{48,56},{56,64},{64,7... | collective-permute-start | bytes 196616 | tf_op jit(solution)/shard_map/while/body/eval_jaxpr/ppermute | solution.py:12
  649.9 13.3 %collective-permute-start.1 = (bf16[2,128,128]{2,1,0:T(8,128)(2,1)S(1)}, bf16[2,128,128]{2,1,0:T(8,128)(2,1)S(1)}, u32[]{:S(2)}, u32[]{:S(2)}) collective-permute-start(bf16[2,128,128]{2,1,0:T(8,128)(2,1)S(1)} %get-tuple-element.318), channel_id=1, source_target_pairs={{0,8},{8,16},{16,24},{24,32},{32,40},{40,48},{48,56},{56,64},{64,7... | collective-permute-start | bytes 196616 | tf_op jit(solution)/shard_map/while/body/eval_jaxpr/ppermute | solution.py:12
  663.9 13.3 %collective-permute-start.1 = (bf16[2,128,128]{2,1,0:T(8,128)(2,1)S(1)}, bf16[2,128,128]{2,1,0:T(8,128)(2,1)S(1)}, u32[]{:S(2)}, u32[]{:S(2)}) collective-permute-start(bf16[2,128,128]{2,1,0:T(8,128)(2,1)S(1)} %get-tuple-element.318), channel_id=1, source_target_pairs={{0,8},{8,16},{16,24},{24,32},{32,40},{40,48},{48,56},{56,64},{64,7... | collective-permute-start | bytes 196616 | tf_op jit(solution)/shard_map/while/body/eval_jaxpr/ppermute | solution.py:12
  677.8 13.3 %collective-permute-start.1 = (bf16[2,128,128]{2,1,0:T(8,128)(2,1)S(1)}, bf16[2,128,128]{2,1,0:T(8,128)(2,1)S(1)}, u32[]{:S(2)}, u32[]{:S(2)}) collective-permute-start(bf16[2,128,128]{2,1,0:T(8,128)(2,1)S(1)} %get-tuple-element.318), channel_id=1, source_target_pairs={{0,8},{8,16},{16,24},{24,32},{32,40},{40,48},{48,56},{56,64},{64,7... | collective-permute-start | bytes 196616 | tf_op jit(solution)/shard_map/while/body/eval_jaxpr/ppermute | solution.py:12
  691.7 13.3 %collective-permute-start.1 = (bf16[2,128,128]{2,1,0:T(8,128)(2,1)S(1)}, bf16[2,128,128]{2,1,0:T(8,128)(2,1)S(1)}, u32[]{:S(2)}, u32[]{:S(2)}) collective-permute-start(bf16[2,128,128]{2,1,0:T(8,128)(2,1)S(1)} %get-tuple-element.318), channel_id=1, source_target_pairs={{0,8},{8,16},{16,24},{24,32},{32,40},{40,48},{48,56},{56,64},{64,7... | collective-permute-start | bytes 196616 | tf_op jit(solution)/shard_map/while/body/eval_jaxpr/ppermute | solution.py:12
  705.6 13.3 %collective-permute-start.1 = (bf16[2,128,128]{2,1,0:T(8,128)(2,1)S(1)}, bf16[2,128,128]{2,1,0:T(8,128)(2,1)S(1)}, u32[]{:S(2)}, u32[]{:S(2)}) collective-permute-start(bf16[2,128,128]{2,1,0:T(8,128)(2,1)S(1)} %get-tuple-element.318), channel_id=1, source_target_pairs={{0,8},{8,16},{16,24},{24,32},{32,40},{40,48},{48,56},{56,64},{64,7... | collective-permute-start | bytes 196616 | tf_op jit(solution)/shard_map/while/body/eval_jaxpr/ppermute | solution.py:12
  719.6 13.3 %collective-permute-start.1 = (bf16[2,128,128]{2,1,0:T(8,128)(2,1)S(1)}, bf16[2,128,128]{2,1,0:T(8,128)(2,1)S(1)}, u32[]{:S(2)}, u32[]{:S(2)}) collective-permute-start(bf16[2,128,128]{2,1,0:T(8,128)(2,1)S(1)} %get-tuple-element.318), channel_id=1, source_target_pairs={{0,8},{8,16},{16,24},{24,32},{32,40},{40,48},{48,56},{56,64},{64,7... | collective-permute-start | bytes 196616 | tf_op jit(solution)/shard_map/while/body/eval_jaxpr/ppermute | solution.py:12
  733.5 13.3 %collective-permute-start.1 = (bf16[2,128,128]{2,1,0:T(8,128)(2,1)S(1)}, bf16[2,128,128]{2,1,0:T(8,128)(2,1)S(1)}, u32[]{:S(2)}, u32[]{:S(2)}) collective-permute-start(bf16[2,128,128]{2,1,0:T(8,128)(2,1)S(1)} %get-tuple-element.318), channel_id=1, source_target_pairs={{0,8},{8,16},{16,24},{24,32},{32,40},{40,48},{48,56},{56,64},{64,7... | collective-permute-start | bytes 196616 | tf_op jit(solution)/shard_map/while/body/eval_jaxpr/ppermute | solution.py:12
  747.4 13.3 %collective-permute-start.1 = (bf16[2,128,128]{2,1,0:T(8,128)(2,1)S(1)}, bf16[2,128,128]{2,1,0:T(8,128)(2,1)S(1)}, u32[]{:S(2)}, u32[]{:S(2)}) collective-permute-start(bf16[2,128,128]{2,1,0:T(8,128)(2,1)S(1)} %get-tuple-element.318), channel_id=1, source_target_pairs={{0,8},{8,16},{16,24},{24,32},{32,40},{40,48},{48,56},{56,64},{64,7... | collective-permute-start | bytes 196616 | tf_op jit(solution)/shard_map/while/body/eval_jaxpr/ppermute | solution.py:12
  761.3 13.3 %collective-permute-start.1 = (bf16[2,128,128]{2,1,0:T(8,128)(2,1)S(1)}, bf16[2,128,128]{2,1,0:T(8,128)(2,1)S(1)}, u32[]{:S(2)}, u32[]{:S(2)}) collective-permute-start(bf16[2,128,128]{2,1,0:T(8,128)(2,1)S(1)} %get-tuple-element.318), channel_id=1, source_target_pairs={{0,8},{8,16},{16,24},{24,32},{32,40},{40,48},{48,56},{56,64},{64,7... | collective-permute-start | bytes 196616 | tf_op jit(solution)/shard_map/while/body/eval_jaxpr/ppermute | solution.py:12
  775.3 13.3 %collective-permute-start.1 = (bf16[2,128,128]{2,1,0:T(8,128)(2,1)S(1)}, bf16[2,128,128]{2,1,0:T(8,128)(2,1)S(1)}, u32[]{:S(2)}, u32[]{:S(2)}) collective-permute-start(bf16[2,128,128]{2,1,0:T(8,128)(2,1)S(1)} %get-tuple-element.318), channel_id=1, source_target_pairs={{0,8},{8,16},{16,24},{24,32},{32,40},{40,48},{48,56},{56,64},{64,7... | collective-permute-start | bytes 196616 | tf_op jit(solution)/shard_map/while/body/eval_jaxpr/ppermute | solution.py:12
  789.2 13.3 %collective-permute-start.1 = (bf16[2,128,128]{2,1,0:T(8,128)(2,1)S(1)}, bf16[2,128,128]{2,1,0:T(8,128)(2,1)S(1)}, u32[]{:S(2)}, u32[]{:S(2)}) collective-permute-start(bf16[2,128,128]{2,1,0:T(8,128)(2,1)S(1)} %get-tuple-element.318), channel_id=1, source_target_pairs={{0,8},{8,16},{16,24},{24,32},{32,40},{40,48},{48,56},{56,64},{64,7... | collective-permute-start | bytes 196616 | tf_op jit(solution)/shard_map/while/body/eval_jaxpr/ppermute | solution.py:12
  803.1 13.3 %collective-permute-start.1 = (bf16[2,128,128]{2,1,0:T(8,128)(2,1)S(1)}, bf16[2,128,128]{2,1,0:T(8,128)(2,1)S(1)}, u32[]{:S(2)}, u32[]{:S(2)}) collective-permute-start(bf16[2,128,128]{2,1,0:T(8,128)(2,1)S(1)} %get-tuple-element.318), channel_id=1, source_target_pairs={{0,8},{8,16},{16,24},{24,32},{32,40},{40,48},{48,56},{56,64},{64,7... | collective-permute-start | bytes 196616 | tf_op jit(solution)/shard_map/while/body/eval_jaxpr/ppermute | solution.py:12
  817.0 13.3 %collective-permute-start.1 = (bf16[2,128,128]{2,1,0:T(8,128)(2,1)S(1)}, bf16[2,128,128]{2,1,0:T(8,128)(2,1)S(1)}, u32[]{:S(2)}, u32[]{:S(2)}) collective-permute-start(bf16[2,128,128]{2,1,0:T(8,128)(2,1)S(1)} %get-tuple-element.318), channel_id=1, source_target_pairs={{0,8},{8,16},{16,24},{24,32},{32,40},{40,48},{48,56},{56,64},{64,7... | collective-permute-start | bytes 196616 | tf_op jit(solution)/shard_map/while/body/eval_jaxpr/ppermute | solution.py:12
  830.9 13.3 %collective-permute-start.1 = (bf16[2,128,128]{2,1,0:T(8,128)(2,1)S(1)}, bf16[2,128,128]{2,1,0:T(8,128)(2,1)S(1)}, u32[]{:S(2)}, u32[]{:S(2)}) collective-permute-start(bf16[2,128,128]{2,1,0:T(8,128)(2,1)S(1)} %get-tuple-element.318), channel_id=1, source_target_pairs={{0,8},{8,16},{16,24},{24,32},{32,40},{40,48},{48,56},{56,64},{64,7... | collective-permute-start | bytes 196616 | tf_op jit(solution)/shard_map/while/body/eval_jaxpr/ppermute | solution.py:12
  844.9 13.3 %collective-permute-start.1 = (bf16[2,128,128]{2,1,0:T(8,128)(2,1)S(1)}, bf16[2,128,128]{2,1,0:T(8,128)(2,1)S(1)}, u32[]{:S(2)}, u32[]{:S(2)}) collective-permute-start(bf16[2,128,128]{2,1,0:T(8,128)(2,1)S(1)} %get-tuple-element.318), channel_id=1, source_target_pairs={{0,8},{8,16},{16,24},{24,32},{32,40},{40,48},{48,56},{56,64},{64,7... | collective-permute-start | bytes 196616 | tf_op jit(solution)/shard_map/while/body/eval_jaxpr/ppermute | solution.py:12
  858.8 13.3 %collective-permute-start.1 = (bf16[2,128,128]{2,1,0:T(8,128)(2,1)S(1)}, bf16[2,128,128]{2,1,0:T(8,128)(2,1)S(1)}, u32[]{:S(2)}, u32[]{:S(2)}) collective-permute-start(bf16[2,128,128]{2,1,0:T(8,128)(2,1)S(1)} %get-tuple-element.318), channel_id=1, source_target_pairs={{0,8},{8,16},{16,24},{24,32},{32,40},{40,48},{48,56},{56,64},{64,7... | collective-permute-start | bytes 196616 | tf_op jit(solution)/shard_map/while/body/eval_jaxpr/ppermute | solution.py:12
  872.7 13.3 %collective-permute-start.1 = (bf16[2,128,128]{2,1,0:T(8,128)(2,1)S(1)}, bf16[2,128,128]{2,1,0:T(8,128)(2,1)S(1)}, u32[]{:S(2)}, u32[]{:S(2)}) collective-permute-start(bf16[2,128,128]{2,1,0:T(8,128)(2,1)S(1)} %get-tuple-element.318), channel_id=1, source_target_pairs={{0,8},{8,16},{16,24},{24,32},{32,40},{40,48},{48,56},{56,64},{64,7... | collective-permute-start | bytes 196616 | tf_op jit(solution)/shard_map/while/body/eval_jaxpr/ppermute | solution.py:12
  886.6 13.3 %collective-permute-start.1 = (bf16[2,128,128]{2,1,0:T(8,128)(2,1)S(1)}, bf16[2,128,128]{2,1,0:T(8,128)(2,1)S(1)}, u32[]{:S(2)}, u32[]{:S(2)}) collective-permute-start(bf16[2,128,128]{2,1,0:T(8,128)(2,1)S(1)} %get-tuple-element.318), channel_id=1, source_target_pairs={{0,8},{8,16},{16,24},{24,32},{32,40},{40,48},{48,56},{56,64},{64,7... | collective-permute-start | bytes 196616 | tf_op jit(solution)/shard_map/while/body/eval_jaxpr/ppermute | solution.py:12
  900.6 13.3 %collective-permute-start.1 = (bf16[2,128,128]{2,1,0:T(8,128)(2,1)S(1)}, bf16[2,128,128]{2,1,0:T(8,128)(2,1)S(1)}, u32[]{:S(2)}, u32[]{:S(2)}) collective-permute-start(bf16[2,128,128]{2,1,0:T(8,128)(2,1)S(1)} %get-tuple-element.318), channel_id=1, source_target_pairs={{0,8},{8,16},{16,24},{24,32},{32,40},{40,48},{48,56},{56,64},{64,7... | collective-permute-start | bytes 196616 | tf_op jit(solution)/shard_map/while/body/eval_jaxpr/ppermute | solution.py:12
  914.5 13.3 %collective-permute-start.1 = (bf16[2,128,128]{2,1,0:T(8,128)(2,1)S(1)}, bf16[2,128,128]{2,1,0:T(8,128)(2,1)S(1)}, u32[]{:S(2)}, u32[]{:S(2)}) collective-permute-start(bf16[2,128,128]{2,1,0:T(8,128)(2,1)S(1)} %get-tuple-element.318), channel_id=1, source_target_pairs={{0,8},{8,16},{16,24},{24,32},{32,40},{40,48},{48,56},{56,64},{64,7... | collective-permute-start | bytes 196616 | tf_op jit(solution)/shard_map/while/body/eval_jaxpr/ppermute | solution.py:12
  928.4 13.3 %collective-permute-start.1 = (bf16[2,128,128]{2,1,0:T(8,128)(2,1)S(1)}, bf16[2,128,128]{2,1,0:T(8,128)(2,1)S(1)}, u32[]{:S(2)}, u32[]{:S(2)}) collective-permute-start(bf16[2,128,128]{2,1,0:T(8,128)(2,1)S(1)} %get-tuple-element.318), channel_id=1, source_target_pairs={{0,8},{8,16},{16,24},{24,32},{32,40},{40,48},{48,56},{56,64},{64,7... | collective-permute-start | bytes 196616 | tf_op jit(solution)/shard_map/while/body/eval_jaxpr/ppermute | solution.py:12
  942.3 13.3 %collective-permute-start.1 = (bf16[2,128,128]{2,1,0:T(8,128)(2,1)S(1)}, bf16[2,128,128]{2,1,0:T(8,128)(2,1)S(1)}, u32[]{:S(2)}, u32[]{:S(2)}) collective-permute-start(bf16[2,128,128]{2,1,0:T(8,128)(2,1)S(1)} %get-tuple-element.318), channel_id=1, source_target_pairs={{0,8},{8,16},{16,24},{24,32},{32,40},{40,48},{48,56},{56,64},{64,7... | collective-permute-start | bytes 196616 | tf_op jit(solution)/shard_map/while/body/eval_jaxpr/ppermute | solution.py:12
  956.3 13.3 %collective-permute-start.1 = (bf16[2,128,128]{2,1,0:T(8,128)(2,1)S(1)}, bf16[2,128,128]{2,1,0:T(8,128)(2,1)S(1)}, u32[]{:S(2)}, u32[]{:S(2)}) collective-permute-start(bf16[2,128,128]{2,1,0:T(8,128)(2,1)S(1)} %get-tuple-element.318), channel_id=1, source_target_pairs={{0,8},{8,16},{16,24},{24,32},{32,40},{40,48},{48,56},{56,64},{64,7... | collective-permute-start | bytes 196616 | tf_op jit(solution)/shard_map/while/body/eval_jaxpr/ppermute | solution.py:12
  970.2 13.3 %collective-permute-start.1 = (bf16[2,128,128]{2,1,0:T(8,128)(2,1)S(1)}, bf16[2,128,128]{2,1,0:T(8,128)(2,1)S(1)}, u32[]{:S(2)}, u32[]{:S(2)}) collective-permute-start(bf16[2,128,128]{2,1,0:T(8,128)(2,1)S(1)} %get-tuple-element.318), channel_id=1, source_target_pairs={{0,8},{8,16},{16,24},{24,32},{32,40},{40,48},{48,56},{56,64},{64,7... | collective-permute-start | bytes 196616 | tf_op jit(solution)/shard_map/while/body/eval_jaxpr/ppermute | solution.py:12
  984.1 13.3 %collective-permute-start.1 = (bf16[2,128,128]{2,1,0:T(8,128)(2,1)S(1)}, bf16[2,128,128]{2,1,0:T(8,128)(2,1)S(1)}, u32[]{:S(2)}, u32[]{:S(2)}) collective-permute-start(bf16[2,128,128]{2,1,0:T(8,128)(2,1)S(1)} %get-tuple-element.318), channel_id=1, source_target_pairs={{0,8},{8,16},{16,24},{24,32},{32,40},{40,48},{48,56},{56,64},{64,7... | collective-permute-start | bytes 196616 | tf_op jit(solution)/shard_map/while/body/eval_jaxpr/ppermute | solution.py:12
  998.0 13.3 %collective-permute-start.1 = (bf16[2,128,128]{2,1,0:T(8,128)(2,1)S(1)}, bf16[2,128,128]{2,1,0:T(8,128)(2,1)S(1)}, u32[]{:S(2)}, u32[]{:S(2)}) collective-permute-start(bf16[2,128,128]{2,1,0:T(8,128)(2,1)S(1)} %get-tuple-element.318), channel_id=1, source_target_pairs={{0,8},{8,16},{16,24},{24,32},{32,40},{40,48},{48,56},{56,64},{64,7... | collective-permute-start | bytes 196616 | tf_op jit(solution)/shard_map/while/body/eval_jaxpr/ppermute | solution.py:12
  1011.9 13.3 %collective-permute-start.1 = (bf16[2,128,128]{2,1,0:T(8,128)(2,1)S(1)}, bf16[2,128,128]{2,1,0:T(8,128)(2,1)S(1)}, u32[]{:S(2)}, u32[]{:S(2)}) collective-permute-start(bf16[2,128,128]{2,1,0:T(8,128)(2,1)S(1)} %get-tuple-element.318), channel_id=1, source_target_pairs={{0,8},{8,16},{16,24},{24,32},{32,40},{40,48},{48,56},{56,64},{64,7... | collective-permute-start | bytes 196616 | tf_op jit(solution)/shard_map/while/body/eval_jaxpr/ppermute | solution.py:12
  1025.9 13.3 %collective-permute-start.1 = (bf16[2,128,128]{2,1,0:T(8,128)(2,1)S(1)}, bf16[2,128,128]{2,1,0:T(8,128)(2,1)S(1)}, u32[]{:S(2)}, u32[]{:S(2)}) collective-permute-start(bf16[2,128,128]{2,1,0:T(8,128)(2,1)S(1)} %get-tuple-element.318), channel_id=1, source_target_pairs={{0,8},{8,16},{16,24},{24,32},{32,40},{40,48},{48,56},{56,64},{64,7... | collective-permute-start | bytes 196616 | tf_op jit(solution)/shard_map/while/body/eval_jaxpr/ppermute | solution.py:12
  (68 other events, 2319.0 us)
Sparse Core Ops, SparseCore 0:
  10.8 85.6 all-gather.2
  98.5 65.5 all-gather.4
where the time goes:
time: 1090 us; the launch traced here: 1080 us
  waiting for transfers between devices  494 us (45%)
  starting transfers between devices  302 us (28%)
  loops' own time  196 us (18%)
  other arithmetic  50.1 us (5%)
  local copies, waits for them, and re-layouts  16.1 us (1%)
  between operations  14.9 us (1%)
  matrix products  11.9 us (1%)
    ppermute x126, waiting for transfers between devices, passed_along(): lax.ppermute(value, axis, [(source, source + steps) for source in range(l...  340 us
    ppermute x126, starting transfers between devices, passed_along(): lax.ppermute(value, axis, [(source, source + steps) for source in range(l...  302 us
    another operation x1, loops' own time, per_device(): lax.fori_loop(0, lax.axis_size('ctx') - 1, hand_round, (own_pair, start_p...  194 us
    all_gather x1, waiting for transfers between devices, per_device(): lax.all_gather(w_qkv, 'ctx', axis=1, tiled=True)  84.4 us
    all_gather x1, waiting for transfers between devices, per_device(): whole = lax.all_gather(tokens, 'head', axis=1, tiled=True)  67.6 us
    add x63, other arithmetic, combine(): later_state + jnp.where(linked, first_state, 0.0)  40.5 us
  transfers between devices with their start and end apart: 128, of which 65 were waited for; matrix products, arithmetic and copies ran while one was open for 0% of the time, Pallas kernels for 0%

commit v1 on v0

--- a/solution.py
+++ b/solution.py
@@ -71,7 +71,9 @@
     projected = jnp.einsum(
         "tr,grc->gtc",
         whole,
-        lax.all_gather(w_qkv, "ctx", axis=1, tiled=True),
+        jnp.concatenate(
+            lax.all_to_all(jnp.stack([w_qkv] * lax.axis_size("ctx")), "ctx", 0, 0), axis=1
+        ),
         preferred_element_type=jnp.float32,
     ).astype(jnp.bfloat16)
     queries, key_map, values, seg_float, kv_state, tail_id = prepare(projected, seg_ids)

time: 1090 us -> 1010 us (0.927)
  the two profiles are of different devices: /device:TPU:32 before, /device:TPU:480 now
where the time goes in v1:
time: 1010 us; the launch traced here: 1000 us
  waiting for transfers between devices  410 us (41%)
  starting transfers between devices  311 us (31%)
  loops' own time  190 us (19%)
  other arithmetic  42.9 us (4%)
  local copies, waits for them, and re-layouts  21 us (2%)
  between operations  14.7 us (1%)
  matrix products  12.1 us (1%)
    ppermute x126, waiting for transfers between devices, passed_along(): lax.ppermute(value, axis, [(source, source + steps) for source in range(l...  342 us
    ppermute x126, starting transfers between devices, passed_along(): lax.ppermute(value, axis, [(source, source + steps) for source in range(l...  300 us
    another operation x1, loops' own time, per_device(): lax.fori_loop(0, lax.axis_size('ctx') - 1, hand_round, (own_pair, start_p...  189 us
    all_to_all x1, waiting for transfers between devices, per_device(): lax.all_to_all(jnp.stack([w_qkv] * lax.axis_size('ctx')), 'ctx', 0, 0)  67.3 us
    add x63, other arithmetic, combine(): later_state + jnp.where(linked, first_state, 0.0)  40.3 us
  transfers between devices with their start and end apart: 128, of which 64 were waited for; matrix products, arithmetic and copies ran while one was open for 1% of the time, Pallas kernels for 0%

profile of v1, /device:TPU:480, one launch (start us, length us, event | category | flops | bytes accessed | tf_op | source)
XLA Modules:
  0.0 1001.6 jit_solution(8587329449426272899)
XLA Ops:
  10.2 10.5 %all-to-all-start = ((bf16[64,3,32,256]{3,2,1,0:T(8,128)(2,1)}), bf16[64,3,32,256]{3,2,1,0:T(8,128)(2,1)S(1)}, u32[]{:S(2)}, u32[]{:S(2)}) async-start(bf16[64,3,32,256]{3,2,1,0:T(8,128)(2,1)} %stack.2), calls=%async_computation | async-start | bytes 6291456 | tf_op jit(solution)/shard_map/all_to_all | solution.py:75
  22.9 67.3 %all-to-all-done = bf16[64,3,32,256]{3,2,1,0:T(8,128)(2,1)S(1)} async-done(((bf16[64,3,32,256]{3,2,1,0:T(8,128)(2,1)}), bf16[64,3,32,256]{3,2,1,0:T(8,128)(2,1)S(1)}, u32[]{:S(2)}, u32[]{:S(2)}) %all-to-all-start) | async-done | bytes 3145760 | tf_op jit(solution)/shard_map/all_to_all | solution.py:75
  92.3 6.6 fusion.15
  102.2 871.6 %while.28 = (s32[]{:T(128)}, bf16[2,128,128]{2,1,0:T(8,128)(2,1)S(1)}, bf16[]{:T(256)}, bf16[2,128,128]{2,1,0:T(8,128)(2,1)}, f32[]{:T(128)}, /*index=5*/f32[]{:...) while((s32[]{:T(128)}, bf16[2,128,128]{2,1,0:T(8,128)(2,1)S(1)}, bf16[]{:T(256)}, ...), condition=%wide.region_3.4_spmd, body=%wide.region_2.3_spmd.sunk | while | flops 163846 | bytes 590031 | solution.py:92
  120.8 5.4 collective-permute-done
  134.6 5.4 collective-permute-done
  148.4 5.4 collective-permute-done
  162.3 5.4 collective-permute-done
  176.1 5.4 collective-permute-done
  189.9 5.4 collective-permute-done
  203.8 5.4 collective-permute-done
  217.6 5.4 collective-permute-done
  231.4 5.4 collective-permute-done
  245.3 5.4 collective-permute-done
  259.1 5.4 collective-permute-done
  272.9 5.4 collective-permute-done
  286.8 5.4 collective-permute-done
  300.6 5.4 collective-permute-done
  314.4 5.4 collective-permute-done
  328.3 5.4 collective-permute-done
  342.1 5.4 collective-permute-done
  355.9 5.4 collective-permute-done
  369.8 5.4 collective-permute-done
  383.6 5.4 collective-permute-done
  397.4 5.4 collective-permute-done
  411.3 5.4 collective-permute-done
  425.1 5.4 collective-permute-done
  439.0 5.4 collective-permute-done
  452.8 5.4 collective-permute-done
  466.6 5.4 collective-permute-done
  480.5 5.4 collective-permute-done
  494.3 5.4 collective-permute-done
  508.1 5.4 collective-permute-done
  522.0 5.4 collective-permute-done
  535.8 5.4 collective-permute-done
  549.6 5.4 collective-permute-done
  563.5 5.4 collective-permute-done
  577.3 5.4 collective-permute-done
  591.1 5.4 collective-permute-done
  605.0 5.4 collective-permute-done
  618.8 5.4 collective-permute-done
  632.6 5.4 collective-permute-done
  646.5 5.4 collective-permute-done
  660.3 5.4 collective-permute-done
  674.1 5.4 collective-permute-done
  688.0 5.4 collective-permute-done
  701.8 5.4 collective-permute-done
  715.6 5.4 collective-permute-done
  729.5 5.4 collective-permute-done
  743.3 5.4 collective-permute-done
  771.0 5.4 collective-permute-done
  798.6 5.4 collective-permute-done
  826.3 5.4 collective-permute-done
  840.1 5.4 collective-permute-done
  854.0 5.4 collective-permute-done
  867.8 5.4 collective-permute-done
  881.6 5.4 collective-permute-done
  895.5 5.4 collective-permute-done
  909.3 5.4 collective-permute-done
  923.1 5.4 collective-permute-done
  937.0 5.4 collective-permute-done
  950.8 5.4 collective-permute-done
  964.7 5.4 collective-permute-done
  973.7 18.5 %while.29 = (s32[]{:T(128)}, f32[2,512,2,128]{1,0,3,2:T(2,128)S(1)}, s32[2]{0:T(128)S(1)}, f32[1024]{0:T(1024)S(1)}, bf16[1024,2,128]{2,0,1:T(8,128)(2,1)S(1)}, ...) while((s32[]{:T(128)}, ...), condition=%wide.region_1.2_spmd.clone, body=%wide.region_0.1_spmd.clone.sunk | while | flops 540541440 | bytes 4995255 | solution.py:62
  (305 shorter events, 392.2 us)
Async XLA Ops:
  6.5 85.8 %all-gather.2.cloned.1.call-start = ((), (), s32[]{:S(2)}) async-start(), calls=%async_computation.1 | async-start | bytes 4718592 | tf_op jit(solution)/shard_map/all_gather | solution.py:70
  10.2 80.1 %all-to-all-start = ((bf16[64,3,32,256]{3,2,1,0:T(8,128)(2,1)}), bf16[64,3,32,256]{3,2,1,0:T(8,128)(2,1)S(1)}, u32[]{:S(2)}, u32[]{:S(2)}) async-start(bf16[64,3,32,256]{3,2,1,0:T(8,128)(2,1)} %stack.2), calls=%async_computation | async-start | bytes 6291456 | tf_op jit(solution)/shard_map/all_to_all | solution.py:75
  102.2 13.2 %collective-permute-start.1 = (bf16[2,128,128]{2,1,0:T(8,128)(2,1)S(1)}, bf16[2,128,128]{2,1,0:T(8,128)(2,1)S(1)}, u32[]{:S(2)}, u32[]{:S(2)}) collective-permute-start(bf16[2,128,128]{2,1,0:T(8,128)(2,1)S(1)} %get-tuple-element.332), channel_id=1, source_target_pairs={{0,8},{8,16},{16,24},{24,32},{32,40},{40,48},{48,56},{56,64},{64,7... | collective-permute-start | bytes 196616 | tf_op jit(solution)/shard_map/while/body/eval_jaxpr/ppermute | solution.py:12
  116.0 13.2 %collective-permute-start.1 = (bf16[2,128,128]{2,1,0:T(8,128)(2,1)S(1)}, bf16[2,128,128]{2,1,0:T(8,128)(2,1)S(1)}, u32[]{:S(2)}, u32[]{:S(2)}) collective-permute-start(bf16[2,128,128]{2,1,0:T(8,128)(2,1)S(1)} %get-tuple-element.332), channel_id=1, source_target_pairs={{0,8},{8,16},{16,24},{24,32},{32,40},{40,48},{48,56},{56,64},{64,7... | collective-permute-start | bytes 196616 | tf_op jit(solution)/shard_map/while/body/eval_jaxpr/ppermute | solution.py:12
  129.8 13.2 %collective-permute-start.1 = (bf16[2,128,128]{2,1,0:T(8,128)(2,1)S(1)}, bf16[2,128,128]{2,1,0:T(8,128)(2,1)S(1)}, u32[]{:S(2)}, u32[]{:S(2)}) collective-permute-start(bf16[2,128,128]{2,1,0:T(8,128)(2,1)S(1)} %get-tuple-element.332), channel_id=1, source_target_pairs={{0,8},{8,16},{16,24},{24,32},{32,40},{40,48},{48,56},{56,64},{64,7... | collective-permute-start | bytes 196616 | tf_op jit(solution)/shard_map/while/body/eval_jaxpr/ppermute | solution.py:12
  143.7 13.2 %collective-permute-start.1 = (bf16[2,128,128]{2,1,0:T(8,128)(2,1)S(1)}, bf16[2,128,128]{2,1,0:T(8,128)(2,1)S(1)}, u32[]{:S(2)}, u32[]{:S(2)}) collective-permute-start(bf16[2,128,128]{2,1,0:T(8,128)(2,1)S(1)} %get-tuple-element.332), channel_id=1, source_target_pairs={{0,8},{8,16},{16,24},{24,32},{32,40},{40,48},{48,56},{56,64},{64,7... | collective-permute-start | bytes 196616 | tf_op jit(solution)/shard_map/while/body/eval_jaxpr/ppermute | solution.py:12
  157.5 13.2 %collective-permute-start.1 = (bf16[2,128,128]{2,1,0:T(8,128)(2,1)S(1)}, bf16[2,128,128]{2,1,0:T(8,128)(2,1)S(1)}, u32[]{:S(2)}, u32[]{:S(2)}) collective-permute-start(bf16[2,128,128]{2,1,0:T(8,128)(2,1)S(1)} %get-tuple-element.332), channel_id=1, source_target_pairs={{0,8},{8,16},{16,24},{24,32},{32,40},{40,48},{48,56},{56,64},{64,7... | collective-permute-start | bytes 196616 | tf_op jit(solution)/shard_map/while/body/eval_jaxpr/ppermute | solution.py:12
  171.3 13.2 %collective-permute-start.1 = (bf16[2,128,128]{2,1,0:T(8,128)(2,1)S(1)}, bf16[2,128,128]{2,1,0:T(8,128)(2,1)S(1)}, u32[]{:S(2)}, u32[]{:S(2)}) collective-permute-start(bf16[2,128,128]{2,1,0:T(8,128)(2,1)S(1)} %get-tuple-element.332), channel_id=1, source_target_pairs={{0,8},{8,16},{16,24},{24,32},{32,40},{40,48},{48,56},{56,64},{64,7... | collective-permute-start | bytes 196616 | tf_op jit(solution)/shard_map/while/body/eval_jaxpr/ppermute | solution.py:12
  185.2 13.2 %collective-permute-start.1 = (bf16[2,128,128]{2,1,0:T(8,128)(2,1)S(1)}, bf16[2,128,128]{2,1,0:T(8,128)(2,1)S(1)}, u32[]{:S(2)}, u32[]{:S(2)}) collective-permute-start(bf16[2,128,128]{2,1,0:T(8,128)(2,1)S(1)} %get-tuple-element.332), channel_id=1, source_target_pairs={{0,8},{8,16},{16,24},{24,32},{32,40},{40,48},{48,56},{56,64},{64,7... | collective-permute-start | bytes 196616 | tf_op jit(solution)/shard_map/while/body/eval_jaxpr/ppermute | solution.py:12
  199.0 13.2 %collective-permute-start.1 = (bf16[2,128,128]{2,1,0:T(8,128)(2,1)S(1)}, bf16[2,128,128]{2,1,0:T(8,128)(2,1)S(1)}, u32[]{:S(2)}, u32[]{:S(2)}) collective-permute-start(bf16[2,128,128]{2,1,0:T(8,128)(2,1)S(1)} %get-tuple-element.332), channel_id=1, source_target_pairs={{0,8},{8,16},{16,24},{24,32},{32,40},{40,48},{48,56},{56,64},{64,7... | collective-permute-start | bytes 196616 | tf_op jit(solution)/shard_map/while/body/eval_jaxpr/ppermute | solution.py:12
  212.8 13.2 %collective-permute-start.1 = (bf16[2,128,128]{2,1,0:T(8,128)(2,1)S(1)}, bf16[2,128,128]{2,1,0:T(8,128)(2,1)S(1)}, u32[]{:S(2)}, u32[]{:S(2)}) collective-permute-start(bf16[2,128,128]{2,1,0:T(8,128)(2,1)S(1)} %get-tuple-element.332), channel_id=1, source_target_pairs={{0,8},{8,16},{16,24},{24,32},{32,40},{40,48},{48,56},{56,64},{64,7... | collective-permute-start | bytes 196616 | tf_op jit(solution)/shard_map/while/body/eval_jaxpr/ppermute | solution.py:12
  226.7 13.2 %collective-permute-start.1 = (bf16[2,128,128]{2,1,0:T(8,128)(2,1)S(1)}, bf16[2,128,128]{2,1,0:T(8,128)(2,1)S(1)}, u32[]{:S(2)}, u32[]{:S(2)}) collective-permute-start(bf16[2,128,128]{2,1,0:T(8,128)(2,1)S(1)} %get-tuple-element.332), channel_id=1, source_target_pairs={{0,8},{8,16},{16,24},{24,32},{32,40},{40,48},{48,56},{56,64},{64,7... | collective-permute-start | bytes 196616 | tf_op jit(solution)/shard_map/while/body/eval_jaxpr/ppermute | solution.py:12
  240.5 13.2 %collective-permute-start.1 = (bf16[2,128,128]{2,1,0:T(8,128)(2,1)S(1)}, bf16[2,128,128]{2,1,0:T(8,128)(2,1)S(1)}, u32[]{:S(2)}, u32[]{:S(2)}) collective-permute-start(bf16[2,128,128]{2,1,0:T(8,128)(2,1)S(1)} %get-tuple-element.332), channel_id=1, source_target_pairs={{0,8},{8,16},{16,24},{24,32},{32,40},{40,48},{48,56},{56,64},{64,7... | collective-permute-start | bytes 196616 | tf_op jit(solution)/shard_map/while/body/eval_jaxpr/ppermute | solution.py:12
  254.3 13.2 %collective-permute-start.1 = (bf16[2,128,128]{2,1,0:T(8,128)(2,1)S(1)}, bf16[2,128,128]{2,1,0:T(8,128)(2,1)S(1)}, u32[]{:S(2)}, u32[]{:S(2)}) collective-permute-start(bf16[2,128,128]{2,1,0:T(8,128)(2,1)S(1)} %get-tuple-element.332), channel_id=1, source_target_pairs={{0,8},{8,16},{16,24},{24,32},{32,40},{40,48},{48,56},{56,64},{64,7... | collective-permute-start | bytes 196616 | tf_op jit(solution)/shard_map/while/body/eval_jaxpr/ppermute | solution.py:12
  268.2 13.2 %collective-permute-start.1 = (bf16[2,128,128]{2,1,0:T(8,128)(2,1)S(1)}, bf16[2,128,128]{2,1,0:T(8,128)(2,1)S(1)}, u32[]{:S(2)}, u32[]{:S(2)}) collective-permute-start(bf16[2,128,128]{2,1,0:T(8,128)(2,1)S(1)} %get-tuple-element.332), channel_id=1, source_target_pairs={{0,8},{8,16},{16,24},{24,32},{32,40},{40,48},{48,56},{56,64},{64,7... | collective-permute-start | bytes 196616 | tf_op jit(solution)/shard_map/while/body/eval_jaxpr/ppermute | solution.py:12
  282.0 13.2 %collective-permute-start.1 = (bf16[2,128,128]{2,1,0:T(8,128)(2,1)S(1)}, bf16[2,128,128]{2,1,0:T(8,128)(2,1)S(1)}, u32[]{:S(2)}, u32[]{:S(2)}) collective-permute-start(bf16[2,128,128]{2,1,0:T(8,128)(2,1)S(1)} %get-tuple-element.332), channel_id=1, source_target_pairs={{0,8},{8,16},{16,24},{24,32},{32,40},{40,48},{48,56},{56,64},{64,7... | collective-permute-start | bytes 196616 | tf_op jit(solution)/shard_map/while/body/eval_jaxpr/ppermute | solution.py:12
  295.8 13.2 %collective-permute-start.1 = (bf16[2,128,128]{2,1,0:T(8,128)(2,1)S(1)}, bf16[2,128,128]{2,1,0:T(8,128)(2,1)S(1)}, u32[]{:S(2)}, u32[]{:S(2)}) collective-permute-start(bf16[2,128,128]{2,1,0:T(8,128)(2,1)S(1)} %get-tuple-element.332), channel_id=1, source_target_pairs={{0,8},{8,16},{16,24},{24,32},{32,40},{40,48},{48,56},{56,64},{64,7... | collective-permute-start | bytes 196616 | tf_op jit(solution)/shard_map/while/body/eval_jaxpr/ppermute | solution.py:12
  309.7 13.2 %collective-permute-start.1 = (bf16[2,128,128]{2,1,0:T(8,128)(2,1)S(1)}, bf16[2,128,128]{2,1,0:T(8,128)(2,1)S(1)}, u32[]{:S(2)}, u32[]{:S(2)}) collective-permute-start(bf16[2,128,128]{2,1,0:T(8,128)(2,1)S(1)} %get-tuple-element.332), channel_id=1, source_target_pairs={{0,8},{8,16},{16,24},{24,32},{32,40},{40,48},{48,56},{56,64},{64,7... | collective-permute-start | bytes 196616 | tf_op jit(solution)/shard_map/while/body/eval_jaxpr/ppermute | solution.py:12
  323.5 13.2 %collective-permute-start.1 = (bf16[2,128,128]{2,1,0:T(8,128)(2,1)S(1)}, bf16[2,128,128]{2,1,0:T(8,128)(2,1)S(1)}, u32[]{:S(2)}, u32[]{:S(2)}) collective-permute-start(bf16[2,128,128]{2,1,0:T(8,128)(2,1)S(1)} %get-tuple-element.332), channel_id=1, source_target_pairs={{0,8},{8,16},{16,24},{24,32},{32,40},{40,48},{48,56},{56,64},{64,7... | collective-permute-start | bytes 196616 | tf_op jit(solution)/shard_map/while/body/eval_jaxpr/ppermute | solution.py:12
  337.3 13.2 %collective-permute-start.1 = (bf16[2,128,128]{2,1,0:T(8,128)(2,1)S(1)}, bf16[2,128,128]{2,1,0:T(8,128)(2,1)S(1)}, u32[]{:S(2)}, u32[]{:S(2)}) collective-permute-start(bf16[2,128,128]{2,1,0:T(8,128)(2,1)S(1)} %get-tuple-element.332), channel_id=1, source_target_pairs={{0,8},{8,16},{16,24},{24,32},{32,40},{40,48},{48,56},{56,64},{64,7... | collective-permute-start | bytes 196616 | tf_op jit(solution)/shard_map/while/body/eval_jaxpr/ppermute | solution.py:12
  351.2 13.2 %collective-permute-start.1 = (bf16[2,128,128]{2,1,0:T(8,128)(2,1)S(1)}, bf16[2,128,128]{2,1,0:T(8,128)(2,1)S(1)}, u32[]{:S(2)}, u32[]{:S(2)}) collective-permute-start(bf16[2,128,128]{2,1,0:T(8,128)(2,1)S(1)} %get-tuple-element.332), channel_id=1, source_target_pairs={{0,8},{8,16},{16,24},{24,32},{32,40},{40,48},{48,56},{56,64},{64,7... | collective-permute-start | bytes 196616 | tf_op jit(solution)/shard_map/while/body/eval_jaxpr/ppermute | solution.py:12
  365.0 13.2 %collective-permute-start.1 = (bf16[2,128,128]{2,1,0:T(8,128)(2,1)S(1)}, bf16[2,128,128]{2,1,0:T(8,128)(2,1)S(1)}, u32[]{:S(2)}, u32[]{:S(2)}) collective-permute-start(bf16[2,128,128]{2,1,0:T(8,128)(2,1)S(1)} %get-tuple-element.332), channel_id=1, source_target_pairs={{0,8},{8,16},{16,24},{24,32},{32,40},{40,48},{48,56},{56,64},{64,7... | collective-permute-start | bytes 196616 | tf_op jit(solution)/shard_map/while/body/eval_jaxpr/ppermute | solution.py:12
  378.8 13.2 %collective-permute-start.1 = (bf16[2,128,128]{2,1,0:T(8,128)(2,1)S(1)}, bf16[2,128,128]{2,1,0:T(8,128)(2,1)S(1)}, u32[]{:S(2)}, u32[]{:S(2)}) collective-permute-start(bf16[2,128,128]{2,1,0:T(8,128)(2,1)S(1)} %get-tuple-element.332), channel_id=1, source_target_pairs={{0,8},{8,16},{16,24},{24,32},{32,40},{40,48},{48,56},{56,64},{64,7... | collective-permute-start | bytes 196616 | tf_op jit(solution)/shard_map/while/body/eval_jaxpr/ppermute | solution.py:12
  392.7 13.2 %collective-permute-start.1 = (bf16[2,128,128]{2,1,0:T(8,128)(2,1)S(1)}, bf16[2,128,128]{2,1,0:T(8,128)(2,1)S(1)}, u32[]{:S(2)}, u32[]{:S(2)}) collective-permute-start(bf16[2,128,128]{2,1,0:T(8,128)(2,1)S(1)} %get-tuple-element.332), channel_id=1, source_target_pairs={{0,8},{8,16},{16,24},{24,32},{32,40},{40,48},{48,56},{56,64},{64,7... | collective-permute-start | bytes 196616 | tf_op jit(solution)/shard_map/while/body/eval_jaxpr/ppermute | solution.py:12
  406.5 13.2 %collective-permute-start.1 = (bf16[2,128,128]{2,1,0:T(8,128)(2,1)S(1)}, bf16[2,128,128]{2,1,0:T(8,128)(2,1)S(1)}, u32[]{:S(2)}, u32[]{:S(2)}) collective-permute-start(bf16[2,128,128]{2,1,0:T(8,128)(2,1)S(1)} %get-tuple-element.332), channel_id=1, source_target_pairs={{0,8},{8,16},{16,24},{24,32},{32,40},{40,48},{48,56},{56,64},{64,7... | collective-permute-start | bytes 196616 | tf_op jit(solution)/shard_map/while/body/eval_jaxpr/ppermute | solution.py:12
  420.3 13.2 %collective-permute-start.1 = (bf16[2,128,128]{2,1,0:T(8,128)(2,1)S(1)}, bf16[2,128,128]{2,1,0:T(8,128)(2,1)S(1)}, u32[]{:S(2)}, u32[]{:S(2)}) collective-permute-start(bf16[2,128,128]{2,1,0:T(8,128)(2,1)S(1)} %get-tuple-element.332), channel_id=1, source_target_pairs={{0,8},{8,16},{16,24},{24,32},{32,40},{40,48},{48,56},{56,64},{64,7... | collective-permute-start | bytes 196616 | tf_op jit(solution)/shard_map/while/body/eval_jaxpr/ppermute | solution.py:12
  434.2 13.2 %collective-permute-start.1 = (bf16[2,128,128]{2,1,0:T(8,128)(2,1)S(1)}, bf16[2,128,128]{2,1,0:T(8,128)(2,1)S(1)}, u32[]{:S(2)}, u32[]{:S(2)}) collective-permute-start(bf16[2,128,128]{2,1,0:T(8,128)(2,1)S(1)} %get-tuple-element.332), channel_id=1, source_target_pairs={{0,8},{8,16},{16,24},{24,32},{32,40},{40,48},{48,56},{56,64},{64,7... | collective-permute-start | bytes 196616 | tf_op jit(solution)/shard_map/while/body/eval_jaxpr/ppermute | solution.py:12
  448.0 13.2 %collective-permute-start.1 = (bf16[2,128,128]{2,1,0:T(8,128)(2,1)S(1)}, bf16[2,128,128]{2,1,0:T(8,128)(2,1)S(1)}, u32[]{:S(2)}, u32[]{:S(2)}) collective-permute-start(bf16[2,128,128]{2,1,0:T(8,128)(2,1)S(1)} %get-tuple-element.332), channel_id=1, source_target_pairs={{0,8},{8,16},{16,24},{24,32},{32,40},{40,48},{48,56},{56,64},{64,7... | collective-permute-start | bytes 196616 | tf_op jit(solution)/shard_map/while/body/eval_jaxpr/ppermute | solution.py:12
  461.8 13.2 %collective-permute-start.1 = (bf16[2,128,128]{2,1,0:T(8,128)(2,1)S(1)}, bf16[2,128,128]{2,1,0:T(8,128)(2,1)S(1)}, u32[]{:S(2)}, u32[]{:S(2)}) collective-permute-start(bf16[2,128,128]{2,1,0:T(8,128)(2,1)S(1)} %get-tuple-element.332), channel_id=1, source_target_pairs={{0,8},{8,16},{16,24},{24,32},{32,40},{40,48},{48,56},{56,64},{64,7... | collective-permute-start | bytes 196616 | tf_op jit(solution)/shard_map/while/body/eval_jaxpr/ppermute | solution.py:12
  475.7 13.2 %collective-permute-start.1 = (bf16[2,128,128]{2,1,0:T(8,128)(2,1)S(1)}, bf16[2,128,128]{2,1,0:T(8,128)(2,1)S(1)}, u32[]{:S(2)}, u32[]{:S(2)}) collective-permute-start(bf16[2,128,128]{2,1,0:T(8,128)(2,1)S(1)} %get-tuple-element.332), channel_id=1, source_target_pairs={{0,8},{8,16},{16,24},{24,32},{32,40},{40,48},{48,56},{56,64},{64,7... | collective-permute-start | bytes 196616 | tf_op jit(solution)/shard_map/while/body/eval_jaxpr/ppermute | solution.py:12
  489.5 13.2 %collective-permute-start.1 = (bf16[2,128,128]{2,1,0:T(8,128)(2,1)S(1)}, bf16[2,128,128]{2,1,0:T(8,128)(2,1)S(1)}, u32[]{:S(2)}, u32[]{:S(2)}) collective-permute-start(bf16[2,128,128]{2,1,0:T(8,128)(2,1)S(1)} %get-tuple-element.332), channel_id=1, source_target_pairs={{0,8},{8,16},{16,24},{24,32},{32,40},{40,48},{48,56},{56,64},{64,7... | collective-permute-start | bytes 196616 | tf_op jit(solution)/shard_map/while/body/eval_jaxpr/ppermute | solution.py:12
  503.3 13.2 %collective-permute-start.1 = (bf16[2,128,128]{2,1,0:T(8,128)(2,1)S(1)}, bf16[2,128,128]{2,1,0:T(8,128)(2,1)S(1)}, u32[]{:S(2)}, u32[]{:S(2)}) collective-permute-start(bf16[2,128,128]{2,1,0:T(8,128)(2,1)S(1)} %get-tuple-element.332), channel_id=1, source_target_pairs={{0,8},{8,16},{16,24},{24,32},{32,40},{40,48},{48,56},{56,64},{64,7... | collective-permute-start | bytes 196616 | tf_op jit(solution)/shard_map/while/body/eval_jaxpr/ppermute | solution.py:12
  517.2 13.2 %collective-permute-start.1 = (bf16[2,128,128]{2,1,0:T(8,128)(2,1)S(1)}, bf16[2,128,128]{2,1,0:T(8,128)(2,1)S(1)}, u32[]{:S(2)}, u32[]{:S(2)}) collective-permute-start(bf16[2,128,128]{2,1,0:T(8,128)(2,1)S(1)} %get-tuple-element.332), channel_id=1, source_target_pairs={{0,8},{8,16},{16,24},{24,32},{32,40},{40,48},{48,56},{56,64},{64,7... | collective-permute-start | bytes 196616 | tf_op jit(solution)/shard_map/while/body/eval_jaxpr/ppermute | solution.py:12
  531.0 13.2 %collective-permute-start.1 = (bf16[2,128,128]{2,1,0:T(8,128)(2,1)S(1)}, bf16[2,128,128]{2,1,0:T(8,128)(2,1)S(1)}, u32[]{:S(2)}, u32[]{:S(2)}) collective-permute-start(bf16[2,128,128]{2,1,0:T(8,128)(2,1)S(1)} %get-tuple-element.332), channel_id=1, source_target_pairs={{0,8},{8,16},{16,24},{24,32},{32,40},{40,48},{48,56},{56,64},{64,7... | collective-permute-start | bytes 196616 | tf_op jit(solution)/shard_map/while/body/eval_jaxpr/ppermute | solution.py:12
  544.9 13.2 %collective-permute-start.1 = (bf16[2,128,128]{2,1,0:T(8,128)(2,1)S(1)}, bf16[2,128,128]{2,1,0:T(8,128)(2,1)S(1)}, u32[]{:S(2)}, u32[]{:S(2)}) collective-permute-start(bf16[2,128,128]{2,1,0:T(8,128)(2,1)S(1)} %get-tuple-element.332), channel_id=1, source_target_pairs={{0,8},{8,16},{16,24},{24,32},{32,40},{40,48},{48,56},{56,64},{64,7... | collective-permute-start | bytes 196616 | tf_op jit(solution)/shard_map/while/body/eval_jaxpr/ppermute | solution.py:12
  558.7 13.2 %collective-permute-start.1 = (bf16[2,128,128]{2,1,0:T(8,128)(2,1)S(1)}, bf16[2,128,128]{2,1,0:T(8,128)(2,1)S(1)}, u32[]{:S(2)}, u32[]{:S(2)}) collective-permute-start(bf16[2,128,128]{2,1,0:T(8,128)(2,1)S(1)} %get-tuple-element.332), channel_id=1, source_target_pairs={{0,8},{8,16},{16,24},{24,32},{32,40},{40,48},{48,56},{56,64},{64,7... | collective-permute-start | bytes 196616 | tf_op jit(solution)/shard_map/while/body/eval_jaxpr/ppermute | solution.py:12
  572.5 13.2 %collective-permute-start.1 = (bf16[2,128,128]{2,1,0:T(8,128)(2,1)S(1)}, bf16[2,128,128]{2,1,0:T(8,128)(2,1)S(1)}, u32[]{:S(2)}, u32[]{:S(2)}) collective-permute-start(bf16[2,128,128]{2,1,0:T(8,128)(2,1)S(1)} %get-tuple-element.332), channel_id=1, source_target_pairs={{0,8},{8,16},{16,24},{24,32},{32,40},{40,48},{48,56},{56,64},{64,7... | collective-permute-start | bytes 196616 | tf_op jit(solution)/shard_map/while/body/eval_jaxpr/ppermute | solution.py:12
  586.4 13.2 %collective-permute-start.1 = (bf16[2,128,128]{2,1,0:T(8,128)(2,1)S(1)}, bf16[2,128,128]{2,1,0:T(8,128)(2,1)S(1)}, u32[]{:S(2)}, u32[]{:S(2)}) collective-permute-start(bf16[2,128,128]{2,1,0:T(8,128)(2,1)S(1)} %get-tuple-element.332), channel_id=1, source_target_pairs={{0,8},{8,16},{16,24},{24,32},{32,40},{40,48},{48,56},{56,64},{64,7... | collective-permute-start | bytes 196616 | tf_op jit(solution)/shard_map/while/body/eval_jaxpr/ppermute | solution.py:12
  600.2 13.2 %collective-permute-start.1 = (bf16[2,128,128]{2,1,0:T(8,128)(2,1)S(1)}, bf16[2,128,128]{2,1,0:T(8,128)(2,1)S(1)}, u32[]{:S(2)}, u32[]{:S(2)}) collective-permute-start(bf16[2,128,128]{2,1,0:T(8,128)(2,1)S(1)} %get-tuple-element.332), channel_id=1, source_target_pairs={{0,8},{8,16},{16,24},{24,32},{32,40},{40,48},{48,56},{56,64},{64,7... | collective-permute-start | bytes 196616 | tf_op jit(solution)/shard_map/while/body/eval_jaxpr/ppermute | solution.py:12
  614.0 13.2 %collective-permute-start.1 = (bf16[2,128,128]{2,1,0:T(8,128)(2,1)S(1)}, bf16[2,128,128]{2,1,0:T(8,128)(2,1)S(1)}, u32[]{:S(2)}, u32[]{:S(2)}) collective-permute-start(bf16[2,128,128]{2,1,0:T(8,128)(2,1)S(1)} %get-tuple-element.332), channel_id=1, source_target_pairs={{0,8},{8,16},{16,24},{24,32},{32,40},{40,48},{48,56},{56,64},{64,7... | collective-permute-start | bytes 196616 | tf_op jit(solution)/shard_map/while/body/eval_jaxpr/ppermute | solution.py:12
  627.9 13.2 %collective-permute-start.1 = (bf16[2,128,128]{2,1,0:T(8,128)(2,1)S(1)}, bf16[2,128,128]{2,1,0:T(8,128)(2,1)S(1)}, u32[]{:S(2)}, u32[]{:S(2)}) collective-permute-start(bf16[2,128,128]{2,1,0:T(8,128)(2,1)S(1)} %get-tuple-element.332), channel_id=1, source_target_pairs={{0,8},{8,16},{16,24},{24,32},{32,40},{40,48},{48,56},{56,64},{64,7... | collective-permute-start | bytes 196616 | tf_op jit(solution)/shard_map/while/body/eval_jaxpr/ppermute | solution.py:12
  641.7 13.2 %collective-permute-start.1 = (bf16[2,128,128]{2,1,0:T(8,128)(2,1)S(1)}, bf16[2,128,128]{2,1,0:T(8,128)(2,1)S(1)}, u32[]{:S(2)}, u32[]{:S(2)}) collective-permute-start(bf16[2,128,128]{2,1,0:T(8,128)(2,1)S(1)} %get-tuple-element.332), channel_id=1, source_target_pairs={{0,8},{8,16},{16,24},{24,32},{32,40},{40,48},{48,56},{56,64},{64,7... | collective-permute-start | bytes 196616 | tf_op jit(solution)/shard_map/while/body/eval_jaxpr/ppermute | solution.py:12
  655.5 13.2 %collective-permute-start.1 = (bf16[2,128,128]{2,1,0:T(8,128)(2,1)S(1)}, bf16[2,128,128]{2,1,0:T(8,128)(2,1)S(1)}, u32[]{:S(2)}, u32[]{:S(2)}) collective-permute-start(bf16[2,128,128]{2,1,0:T(8,128)(2,1)S(1)} %get-tuple-element.332), channel_id=1, source_target_pairs={{0,8},{8,16},{16,24},{24,32},{32,40},{40,48},{48,56},{56,64},{64,7... | collective-permute-start | bytes 196616 | tf_op jit(solution)/shard_map/while/body/eval_jaxpr/ppermute | solution.py:12
  669.4 13.2 %collective-permute-start.1 = (bf16[2,128,128]{2,1,0:T(8,128)(2,1)S(1)}, bf16[2,128,128]{2,1,0:T(8,128)(2,1)S(1)}, u32[]{:S(2)}, u32[]{:S(2)}) collective-permute-start(bf16[2,128,128]{2,1,0:T(8,128)(2,1)S(1)} %get-tuple-element.332), channel_id=1, source_target_pairs={{0,8},{8,16},{16,24},{24,32},{32,40},{40,48},{48,56},{56,64},{64,7... | collective-permute-start | bytes 196616 | tf_op jit(solution)/shard_map/while/body/eval_jaxpr/ppermute | solution.py:12
  683.2 13.2 %collective-permute-start.1 = (bf16[2,128,128]{2,1,0:T(8,128)(2,1)S(1)}, bf16[2,128,128]{2,1,0:T(8,128)(2,1)S(1)}, u32[]{:S(2)}, u32[]{:S(2)}) collective-permute-start(bf16[2,128,128]{2,1,0:T(8,128)(2,1)S(1)} %get-tuple-element.332), channel_id=1, source_target_pairs={{0,8},{8,16},{16,24},{24,32},{32,40},{40,48},{48,56},{56,64},{64,7... | collective-permute-start | bytes 196616 | tf_op jit(solution)/shard_map/while/body/eval_jaxpr/ppermute | solution.py:12
  697.0 13.2 %collective-permute-start.1 = (bf16[2,128,128]{2,1,0:T(8,128)(2,1)S(1)}, bf16[2,128,128]{2,1,0:T(8,128)(2,1)S(1)}, u32[]{:S(2)}, u32[]{:S(2)}) collective-permute-start(bf16[2,128,128]{2,1,0:T(8,128)(2,1)S(1)} %get-tuple-element.332), channel_id=1, source_target_pairs={{0,8},{8,16},{16,24},{24,32},{32,40},{40,48},{48,56},{56,64},{64,7... | collective-permute-start | bytes 196616 | tf_op jit(solution)/shard_map/while/body/eval_jaxpr/ppermute | solution.py:12
  710.9 13.2 %collective-permute-start.1 = (bf16[2,128,128]{2,1,0:T(8,128)(2,1)S(1)}, bf16[2,128,128]{2,1,0:T(8,128)(2,1)S(1)}, u32[]{:S(2)}, u32[]{:S(2)}) collective-permute-start(bf16[2,128,128]{2,1,0:T(8,128)(2,1)S(1)} %get-tuple-element.332), channel_id=1, source_target_pairs={{0,8},{8,16},{16,24},{24,32},{32,40},{40,48},{48,56},{56,64},{64,7... | collective-permute-start | bytes 196616 | tf_op jit(solution)/shard_map/while/body/eval_jaxpr/ppermute | solution.py:12
  724.7 13.2 %collective-permute-start.1 = (bf16[2,128,128]{2,1,0:T(8,128)(2,1)S(1)}, bf16[2,128,128]{2,1,0:T(8,128)(2,1)S(1)}, u32[]{:S(2)}, u32[]{:S(2)}) collective-permute-start(bf16[2,128,128]{2,1,0:T(8,128)(2,1)S(1)} %get-tuple-element.332), channel_id=1, source_target_pairs={{0,8},{8,16},{16,24},{24,32},{32,40},{40,48},{48,56},{56,64},{64,7... | collective-permute-start | bytes 196616 | tf_op jit(solution)/shard_map/while/body/eval_jaxpr/ppermute | solution.py:12
  738.5 13.2 %collective-permute-start.1 = (bf16[2,128,128]{2,1,0:T(8,128)(2,1)S(1)}, bf16[2,128,128]{2,1,0:T(8,128)(2,1)S(1)}, u32[]{:S(2)}, u32[]{:S(2)}) collective-permute-start(bf16[2,128,128]{2,1,0:T(8,128)(2,1)S(1)} %get-tuple-element.332), channel_id=1, source_target_pairs={{0,8},{8,16},{16,24},{24,32},{32,40},{40,48},{48,56},{56,64},{64,7... | collective-permute-start | bytes 196616 | tf_op jit(solution)/shard_map/while/body/eval_jaxpr/ppermute | solution.py:12
  752.4 13.2 %collective-permute-start.1 = (bf16[2,128,128]{2,1,0:T(8,128)(2,1)S(1)}, bf16[2,128,128]{2,1,0:T(8,128)(2,1)S(1)}, u32[]{:S(2)}, u32[]{:S(2)}) collective-permute-start(bf16[2,128,128]{2,1,0:T(8,128)(2,1)S(1)} %get-tuple-element.332), channel_id=1, source_target_pairs={{0,8},{8,16},{16,24},{24,32},{32,40},{40,48},{48,56},{56,64},{64,7... | collective-permute-start | bytes 196616 | tf_op jit(solution)/shard_map/while/body/eval_jaxpr/ppermute | solution.py:12
  766.2 13.2 %collective-permute-start.1 = (bf16[2,128,128]{2,1,0:T(8,128)(2,1)S(1)}, bf16[2,128,128]{2,1,0:T(8,128)(2,1)S(1)}, u32[]{:S(2)}, u32[]{:S(2)}) collective-permute-start(bf16[2,128,128]{2,1,0:T(8,128)(2,1)S(1)} %get-tuple-element.332), channel_id=1, source_target_pairs={{0,8},{8,16},{16,24},{24,32},{32,40},{40,48},{48,56},{56,64},{64,7... | collective-permute-start | bytes 196616 | tf_op jit(solution)/shard_map/while/body/eval_jaxpr/ppermute | solution.py:12
  780.0 13.2 %collective-permute-start.1 = (bf16[2,128,128]{2,1,0:T(8,128)(2,1)S(1)}, bf16[2,128,128]{2,1,0:T(8,128)(2,1)S(1)}, u32[]{:S(2)}, u32[]{:S(2)}) collective-permute-start(bf16[2,128,128]{2,1,0:T(8,128)(2,1)S(1)} %get-tuple-element.332), channel_id=1, source_target_pairs={{0,8},{8,16},{16,24},{24,32},{32,40},{40,48},{48,56},{56,64},{64,7... | collective-permute-start | bytes 196616 | tf_op jit(solution)/shard_map/while/body/eval_jaxpr/ppermute | solution.py:12
  793.9 13.2 %collective-permute-start.1 = (bf16[2,128,128]{2,1,0:T(8,128)(2,1)S(1)}, bf16[2,128,128]{2,1,0:T(8,128)(2,1)S(1)}, u32[]{:S(2)}, u32[]{:S(2)}) collective-permute-start(bf16[2,128,128]{2,1,0:T(8,128)(2,1)S(1)} %get-tuple-element.332), channel_id=1, source_target_pairs={{0,8},{8,16},{16,24},{24,32},{32,40},{40,48},{48,56},{56,64},{64,7... | collective-permute-start | bytes 196616 | tf_op jit(solution)/shard_map/while/body/eval_jaxpr/ppermute | solution.py:12
  807.7 13.2 %collective-permute-start.1 = (bf16[2,128,128]{2,1,0:T(8,128)(2,1)S(1)}, bf16[2,128,128]{2,1,0:T(8,128)(2,1)S(1)}, u32[]{:S(2)}, u32[]{:S(2)}) collective-permute-start(bf16[2,128,128]{2,1,0:T(8,128)(2,1)S(1)} %get-tuple-element.332), channel_id=1, source_target_pairs={{0,8},{8,16},{16,24},{24,32},{32,40},{40,48},{48,56},{56,64},{64,7... | collective-permute-start | bytes 196616 | tf_op jit(solution)/shard_map/while/body/eval_jaxpr/ppermute | solution.py:12
  821.5 13.2 %collective-permute-start.1 = (bf16[2,128,128]{2,1,0:T(8,128)(2,1)S(1)}, bf16[2,128,128]{2,1,0:T(8,128)(2,1)S(1)}, u32[]{:S(2)}, u32[]{:S(2)}) collective-permute-start(bf16[2,128,128]{2,1,0:T(8,128)(2,1)S(1)} %get-tuple-element.332), channel_id=1, source_target_pairs={{0,8},{8,16},{16,24},{24,32},{32,40},{40,48},{48,56},{56,64},{64,7... | collective-permute-start | bytes 196616 | tf_op jit(solution)/shard_map/while/body/eval_jaxpr/ppermute | solution.py:12
  835.4 13.2 %collective-permute-start.1 = (bf16[2,128,128]{2,1,0:T(8,128)(2,1)S(1)}, bf16[2,128,128]{2,1,0:T(8,128)(2,1)S(1)}, u32[]{:S(2)}, u32[]{:S(2)}) collective-permute-start(bf16[2,128,128]{2,1,0:T(8,128)(2,1)S(1)} %get-tuple-element.332), channel_id=1, source_target_pairs={{0,8},{8,16},{16,24},{24,32},{32,40},{40,48},{48,56},{56,64},{64,7... | collective-permute-start | bytes 196616 | tf_op jit(solution)/shard_map/while/body/eval_jaxpr/ppermute | solution.py:12
  849.2 13.2 %collective-permute-start.1 = (bf16[2,128,128]{2,1,0:T(8,128)(2,1)S(1)}, bf16[2,128,128]{2,1,0:T(8,128)(2,1)S(1)}, u32[]{:S(2)}, u32[]{:S(2)}) collective-permute-start(bf16[2,128,128]{2,1,0:T(8,128)(2,1)S(1)} %get-tuple-element.332), channel_id=1, source_target_pairs={{0,8},{8,16},{16,24},{24,32},{32,40},{40,48},{48,56},{56,64},{64,7... | collective-permute-start | bytes 196616 | tf_op jit(solution)/shard_map/while/body/eval_jaxpr/ppermute | solution.py:12
  863.0 13.2 %collective-permute-start.1 = (bf16[2,128,128]{2,1,0:T(8,128)(2,1)S(1)}, bf16[2,128,128]{2,1,0:T(8,128)(2,1)S(1)}, u32[]{:S(2)}, u32[]{:S(2)}) collective-permute-start(bf16[2,128,128]{2,1,0:T(8,128)(2,1)S(1)} %get-tuple-element.332), channel_id=1, source_target_pairs={{0,8},{8,16},{16,24},{24,32},{32,40},{40,48},{48,56},{56,64},{64,7... | collective-permute-start | bytes 196616 | tf_op jit(solution)/shard_map/while/body/eval_jaxpr/ppermute | solution.py:12
  876.9 13.2 %collective-permute-start.1 = (bf16[2,128,128]{2,1,0:T(8,128)(2,1)S(1)}, bf16[2,128,128]{2,1,0:T(8,128)(2,1)S(1)}, u32[]{:S(2)}, u32[]{:S(2)}) collective-permute-start(bf16[2,128,128]{2,1,0:T(8,128)(2,1)S(1)} %get-tuple-element.332), channel_id=1, source_target_pairs={{0,8},{8,16},{16,24},{24,32},{32,40},{40,48},{48,56},{56,64},{64,7... | collective-permute-start | bytes 196616 | tf_op jit(solution)/shard_map/while/body/eval_jaxpr/ppermute | solution.py:12
  890.7 13.2 %collective-permute-start.1 = (bf16[2,128,128]{2,1,0:T(8,128)(2,1)S(1)}, bf16[2,128,128]{2,1,0:T(8,128)(2,1)S(1)}, u32[]{:S(2)}, u32[]{:S(2)}) collective-permute-start(bf16[2,128,128]{2,1,0:T(8,128)(2,1)S(1)} %get-tuple-element.332), channel_id=1, source_target_pairs={{0,8},{8,16},{16,24},{24,32},{32,40},{40,48},{48,56},{56,64},{64,7... | collective-permute-start | bytes 196616 | tf_op jit(solution)/shard_map/while/body/eval_jaxpr/ppermute | solution.py:12
  904.5 13.2 %collective-permute-start.1 = (bf16[2,128,128]{2,1,0:T(8,128)(2,1)S(1)}, bf16[2,128,128]{2,1,0:T(8,128)(2,1)S(1)}, u32[]{:S(2)}, u32[]{:S(2)}) collective-permute-start(bf16[2,128,128]{2,1,0:T(8,128)(2,1)S(1)} %get-tuple-element.332), channel_id=1, source_target_pairs={{0,8},{8,16},{16,24},{24,32},{32,40},{40,48},{48,56},{56,64},{64,7... | collective-permute-start | bytes 196616 | tf_op jit(solution)/shard_map/while/body/eval_jaxpr/ppermute | solution.py:12
  918.4 13.2 %collective-permute-start.1 = (bf16[2,128,128]{2,1,0:T(8,128)(2,1)S(1)}, bf16[2,128,128]{2,1,0:T(8,128)(2,1)S(1)}, u32[]{:S(2)}, u32[]{:S(2)}) collective-permute-start(bf16[2,128,128]{2,1,0:T(8,128)(2,1)S(1)} %get-tuple-element.332), channel_id=1, source_target_pairs={{0,8},{8,16},{16,24},{24,32},{32,40},{40,48},{48,56},{56,64},{64,7... | collective-permute-start | bytes 196616 | tf_op jit(solution)/shard_map/while/body/eval_jaxpr/ppermute | solution.py:12
  932.2 13.2 %collective-permute-start.1 = (bf16[2,128,128]{2,1,0:T(8,128)(2,1)S(1)}, bf16[2,128,128]{2,1,0:T(8,128)(2,1)S(1)}, u32[]{:S(2)}, u32[]{:S(2)}) collective-permute-start(bf16[2,128,128]{2,1,0:T(8,128)(2,1)S(1)} %get-tuple-element.332), channel_id=1, source_target_pairs={{0,8},{8,16},{16,24},{24,32},{32,40},{40,48},{48,56},{56,64},{64,7... | collective-permute-start | bytes 196616 | tf_op jit(solution)/shard_map/while/body/eval_jaxpr/ppermute | solution.py:12
  946.0 13.2 %collective-permute-start.1 = (bf16[2,128,128]{2,1,0:T(8,128)(2,1)S(1)}, bf16[2,128,128]{2,1,0:T(8,128)(2,1)S(1)}, u32[]{:S(2)}, u32[]{:S(2)}) collective-permute-start(bf16[2,128,128]{2,1,0:T(8,128)(2,1)S(1)} %get-tuple-element.332), channel_id=1, source_target_pairs={{0,8},{8,16},{16,24},{24,32},{32,40},{40,48},{48,56},{56,64},{64,7... | collective-permute-start | bytes 196616 | tf_op jit(solution)/shard_map/while/body/eval_jaxpr/ppermute | solution.py:12
  (70 other events, 2311.9 us)
Sparse Core Ops, SparseCore 0:
  9.4 63.3 all-gather.1
